TPU v7x, 128 devices: a whole 4x4x4 slice. The times are simulated.
128 devices in a mesh: rad: 4 (over x_hi, core), sec: 32 (over x_lo, y, z).
Axes of the slice: x: 4 (x_hi: 2, x_lo: 2; x = x_hi * 2 + x_lo), y: 4, z: 4, core: 2. Of those that a mesh axis runs over, the one named last changes fastest.
Arguments:
- gas_fields: float32 [5, 128, 16, 8192], P(None, 'rad', None, 'sec'), may hold values from -8 to 8, as said below
- orbit_shift: int32 [128], P('rad'), may hold values from 0 to 8191
- particle_velocity: float32 [3, 524288], P(None, ('rad', 'sec')), may hold values from -6 to 6
- particle_mass: float32 [524288], P(('rad', 'sec')), may hold values from 0.2 to 2
- particle_stop: float32 [524288], P(('rad', 'sec')), may hold values from 0.1 to 10
- particle_cell: int32 [524288], P(('rad', 'sec')), may hold values from 0 to 131071
- particle_dest: int32 [524288, 1], P(('rad', 'sec')), may hold values from 0 to 127; in each aligned block of 4096 rows (0 to 4095, 4096 to 8191, ...) at most 64 rows name the same one
Outputs:
- gas_next: float32 [5, 128, 16, 8192], P(None, 'rad', None, 'sec')
- arrived_velocity: float32 [3, 1048576], P(None, ('rad', 'sec'))
Inputs may be any that keep to these rules, and one draw needn't show every extreme that they name: `gas_fields`: field 0 (density) lies between 0.25 and 4 and momentum over density between -2 and 2. `particle_dest`: among the 4096 particles of one device at most 64 name the same destination; in every draw some device sends exactly 64 to one destination.
All inputs are finite; a program needn't handle non-finite values.
Results may differ from a plain program's by a relative error of at most 0.0003.
Values sent between devices are 32-bit elements; how exact they have to be, the bound alone decides.
No kernel may reach another device: no remote copies, remote signals or barrier semaphores. Data moves between devices by JAX's collectives and lax.ppermute only.
A program may use at most 128 MiB of HBM per device.

v0:
```python
import jax
import jax.numpy as jnp
from jax import lax
from jax.sharding import PartitionSpec as P
from jax.experimental import pallas as pl
from jax.experimental.pallas import tpu as pltpu

sound_speed = 1.0
radial_rate = 0.2
azimuth_rate = 0.2
exact = lax.Precision.HIGHEST


def passed_along(block, axis, distance):
    devices = range(lax.axis_size(axis))
    route = [((i - distance) % len(devices), i) for i in devices]
    return lax.ppermute(block, axis, route)


def with_halo(cells, sides, width, closed):
    for axis, dim in sides:
        count = lax.axis_size(axis)
        ends = count if closed else count - 1
        head = lax.slice_in_dim(cells, 0, width, axis=dim)
        tail = lax.slice_in_dim(cells, cells.shape[dim] - width, cells.shape[dim], axis=dim)
        cells = jnp.concatenate(
            [
                lax.ppermute(tail, axis, [(i, (i + 1) % count) for i in range(ends)]),
                cells,
                lax.ppermute(head, axis, [((i + 1) % count, i) for i in range(ends)]),
            ],
            axis=dim,
        )
    return cells


def limited_slope(left_step, right_step):
    return (
        0.5
        * (jnp.sign(left_step) + jnp.sign(right_step))
        * jnp.minimum(jnp.abs(left_step), jnp.abs(right_step))
    )


def plm_divergence(values, speed, along_axis, extent):

    def take_range(source, offset_at, length):
        return lax.slice_in_dim(source, offset_at, offset_at + length, axis=along_axis)

    left_step = take_range(values, 1, extent + 2) - take_range(values, 0, extent + 2)
    right_step = take_range(values, 2, extent + 2) - take_range(values, 1, extent + 2)
    slopes = limited_slope(left_step, right_step)
    centre = take_range(values, 1, extent + 2)
    left_value = take_range(centre, 0, extent + 1) + 0.5 * take_range(slopes, 0, extent + 1)
    right_value = take_range(centre, 1, extent + 1) - 0.5 * take_range(slopes, 1, extent + 1)
    face_speed = 0.5 * (take_range(speed, 1, extent + 1) + take_range(speed, 2, extent + 1))
    face_flux = face_speed * 0.5 * (left_value + right_value) - 0.5 * (
        jnp.abs(face_speed) + sound_speed
    ) * (right_value - left_value)
    return take_range(face_flux, 1, extent) - take_range(face_flux, 0, extent)


def sector_roll(ring, quotient, remainder):
    sectors, per_member, rows, sector = ring.shape

    def kernel(quotient_ref, remainder_ref, ring_ref, out_ref):
        for i in range(per_member):
            whole = quotient_ref[i]
            part = remainder_ref[i]

            def body(s, carry):
                current = ring_ref[(s - whole + sectors) % sectors, i]
                preceding = ring_ref[(s - whole - 1 + 2 * sectors) % sectors, i]
                window = jnp.concatenate([preceding, current], axis=-1)
                out_ref[s, i] = pltpu.roll(window, part, 1)[:, sector:]
                return carry

            lax.fori_loop(0, sectors, body, 0)

    return pl.pallas_call(
        kernel,
        out_shape=jax.ShapeDtypeStruct(ring.shape, ring.dtype),
        in_specs=[
            pl.BlockSpec(memory_space=pltpu.SMEM),
            pl.BlockSpec(memory_space=pltpu.SMEM),
            pl.BlockSpec(memory_space=pltpu.VMEM),
        ],
        out_specs=pl.BlockSpec(memory_space=pltpu.VMEM),
    )(quotient, remainder, ring)


def sign_of(x):
    return jnp.where(x > 0, 1.0, jnp.where(x < 0, -1.0, 0.0))

def minmod(a, b):
    return 0.5 * (sign_of(a) + sign_of(b)) * jnp.minimum(jnp.abs(a), jnp.abs(b))

def face_divergence(v_m2, v_m1, v0, v_p1, v_p2, s_m1, s0, s_p1):
    slope_m1 = minmod(v_m1 - v_m2, v0 - v_m1)
    slope_0 = minmod(v0 - v_m1, v_p1 - v0)
    slope_p1 = minmod(v_p1 - v0, v_p2 - v_p1)
    def flux(left, right, w):
        return w * 0.5 * (left + right) - 0.5 * (jnp.abs(w) + 1.0) * (right - left)
    upper = flux(v0 + 0.5 * slope_0, v_p1 - 0.5 * slope_p1, 0.5 * (s0 + s_p1))
    lower = flux(v_m1 + 0.5 * slope_m1, v0 - 0.5 * slope_0, 0.5 * (s_m1 + s0))
    return upper - lower

def transport(dragged, speeds, radial_low, radial_high, ring_low, ring_high, rate_r, rate_a):
    fields, radii, layers, cells = dragged.shape

    def kernel(d_ref, s_ref, rl_ref, rh_ref, al_ref, ah_ref, out_ref):
        lane = lax.broadcasted_iota(jnp.int32, (layers, cells), 1)

        def radial_at(f, r, offset):
            k = r + offset
            inner = d_ref[f, jnp.clip(k, 0, radii - 1)] if f < fields else s_ref[0, jnp.clip(k, 0, radii - 1)]
            low = rl_ref[f, jnp.clip(k + 2, 0, 1)]
            high = rh_ref[f, jnp.clip(k - radii, 0, 1)]
            return jnp.where(k < 0, low, jnp.where(k >= radii, high, inner))

        def ring_at(centre, f, r, offset):
            if offset < 0:
                moved = pltpu.roll(centre, -offset, 1)
                for j in range(-offset):
                    edge = al_ref[f, r, :, 2 + offset + j : 3 + offset + j]
                    moved = jnp.where(lane == j, edge, moved)
            else:
                moved = pltpu.roll(centre, cells - offset, 1)
                for j in range(offset):
                    edge = ah_ref[f, r, :, j : j + 1]
                    moved = jnp.where(lane == cells - offset + j, edge, moved)
            return moved

        def body(r, carry):
            sr = s_ref[0, r]
            sa = s_ref[1, r]
            sr_m1 = radial_at(fields, r, -1)
            sr_p1 = radial_at(fields, r, 1)
            sa_m1 = ring_at(sa, fields + 1, r, -1)
            sa_p1 = ring_at(sa, fields + 1, r, 1)
            for f in range(fields):
                v0 = d_ref[f, r]
                radial = face_divergence(
                    radial_at(f, r, -2), radial_at(f, r, -1), v0, radial_at(f, r, 1), radial_at(f, r, 2),
                    sr_m1, sr, sr_p1,
                )
                azimuthal = face_divergence(
                    ring_at(v0, f, r, -2), ring_at(v0, f, r, -1), v0, ring_at(v0, f, r, 1), ring_at(v0, f, r, 2),
                    sa_m1, sa, sa_p1,
                )
                out_ref[f, r] = v0 - rate_r * radial - rate_a * azimuthal
            return carry

        lax.fori_loop(0, radii, body, 0)

    vmem = pl.BlockSpec(memory_space=pltpu.VMEM)
    return pl.pallas_call(
        kernel,
        out_shape=jax.ShapeDtypeStruct(dragged.shape, dragged.dtype),
        in_specs=[vmem] * 6,
        out_specs=vmem,
    )(dragged, speeds, radial_low, radial_high, ring_low, ring_high)


def local(
    gas_fields,
    orbit_shift,
    particle_velocity,
    particle_mass,
    particle_stop,
    particle_cell,
    particle_dest,
):
    field_count, radius_count, layers, sector = gas_fields.shape
    sectors = lax.axis_size("sec")
    per_member = radius_count // sectors
    member = lax.axis_index("sec")
    by_radius = gas_fields.transpose(1, 0, 2, 3)
    ring = lax.all_to_all(by_radius, "sec", split_axis=0, concat_axis=0, tiled=True)
    ring = ring.reshape(sectors, per_member, field_count * layers, sector)
    own_shift = lax.dynamic_slice_in_dim(orbit_shift, member * per_member, per_member)
    rolled = sector_roll(ring, own_shift // sector, own_shift % sector)
    rolled = rolled.reshape(sectors * per_member, field_count, layers, sector)
    shifted = lax.all_to_all(rolled, "sec", split_axis=0, concat_axis=0, tiled=True)
    shifted = shifted.transpose(1, 0, 2, 3)
    per_device = particle_dest.shape[0]
    devices = lax.axis_size(("rad", "sec"))
    capacity = 2 * per_device // devices
    target = particle_dest[:, 0]
    hits = target[:, None] == jnp.arange(devices, dtype=jnp.int32)[None, :]
    block_rows = min(128, per_device)
    block_count = per_device // block_rows
    hit_blocks = hits.astype(jnp.bfloat16).reshape(block_count, block_rows, devices)
    row_index = jnp.arange(block_rows, dtype=jnp.int32)
    within = (row_index[:, None] >= row_index[None, :]).astype(jnp.bfloat16)
    block_index = jnp.arange(block_count, dtype=jnp.int32)
    before = (block_index[:, None] > block_index[None, :]).astype(jnp.bfloat16)
    block_totals = jnp.sum(hit_blocks, axis=1, dtype=jnp.float32).astype(jnp.bfloat16)
    running = jnp.einsum(
        "ij,bjd->bid", within, hit_blocks, preferred_element_type=jnp.float32
    ) + jnp.dot(before, block_totals, preferred_element_type=jnp.float32)[:, None, :]
    running = running.reshape(per_device, devices)
    slot = jnp.sum(jnp.where(hits, running, 0.0), axis=1).astype(jnp.int32) - 1
    records = jnp.concatenate(
        [
            particle_velocity,
            particle_mass[None],
            particle_stop[None],
            particle_cell[None].astype(jnp.float32),
        ],
        axis=0,
    )
    slot_hot = slot[:, None] == jnp.arange(capacity, dtype=jnp.int32)[None, :]
    spread_records = jnp.where(slot_hot[:, None, :], records.T[:, :, None], 0.0).reshape(
        per_device, 6 * capacity
    )
    outbox = jnp.dot(
        hits.astype(jnp.float32).T, spread_records, precision=exact, preferred_element_type=jnp.float32
    ).reshape(devices, 6, capacity)
    inbox = lax.all_to_all(outbox, ("rad", "sec"), split_axis=0, concat_axis=0, tiled=True)
    received = inbox.transpose(1, 0, 2).reshape(6, devices * capacity)
    row_count = radius_count * layers
    velocity_rows = (
        (shifted[1:4] / shifted[0:1])
        .reshape(3, row_count, sector)
        .transpose(1, 0, 2)
        .reshape(row_count, 3 * sector)
    )
    cells = received[5].astype(jnp.int32)
    row_hot = (
        (cells // sector)[:, None] == jnp.arange(row_count, dtype=jnp.int32)[None, :]
    ).astype(jnp.float32)
    azimuth_hot = (
        (cells % sector)[:, None] == jnp.arange(sector, dtype=jnp.int32)[None, :]
    ).astype(jnp.float32)
    picked = jnp.dot(
        row_hot, velocity_rows, precision=lax.Precision.HIGH, preferred_element_type=jnp.float32
    ).reshape(-1, 3, sector)
    local_speed = jnp.sum(picked * azimuth_hot[:, None, :], axis=2).T
    velocity_in = received[0:3]
    fraction = received[4] / (1.0 + received[4])
    change = (velocity_in - local_speed) * fraction[None]
    arrived_velocity = velocity_in - change
    impulse = received[3][None] * change
    spread = (impulse.T[:, :, None] * azimuth_hot[:, None, :]).reshape(-1, 3 * sector)
    deposit_rows = jnp.dot(row_hot.T, spread, precision=lax.Precision.HIGH, preferred_element_type=jnp.float32)
    momentum_added = (
        deposit_rows.reshape(row_count, 3, sector)
        .transpose(1, 0, 2)
        .reshape(3, radius_count, layers, sector)
    )
    dragged = jnp.concatenate([shifted[0:1], shifted[1:4] + momentum_added, shifted[4:5]], axis=0)
    radial_speed = dragged[1] / dragged[0]
    azimuthal_speed = dragged[2] / dragged[0]
    speeds = jnp.stack([radial_speed, azimuthal_speed], axis=0)
    rads = lax.axis_size("rad")
    radial_low = lax.ppermute(
        jnp.concatenate([dragged[:, -2:], speeds[:, -2:]], axis=0),
        "rad",
        [(i, i + 1) for i in range(rads - 1)],
    )
    radial_high = lax.ppermute(
        jnp.concatenate([dragged[:, :2], speeds[:, :2]], axis=0),
        "rad",
        [(i + 1, i) for i in range(rads - 1)],
    )
    ring_low = lax.ppermute(
        jnp.concatenate([dragged[..., -2:], speeds[..., -2:]], axis=0),
        "sec",
        [(i, (i + 1) % sectors) for i in range(sectors)],
    )
    ring_high = lax.ppermute(
        jnp.concatenate([dragged[..., :2], speeds[..., :2]], axis=0),
        "sec",
        [((i + 1) % sectors, i) for i in range(sectors)],
    )
    gas_next = transport(
        dragged, speeds, radial_low, radial_high, ring_low, ring_high, radial_rate, azimuth_rate
    )
    return (gas_next, arrived_velocity)


def solution(mesh):
    placed = (
        P(None, "rad", None, "sec"),
        P("rad"),
        P(None, ("rad", "sec")),
        P(("rad", "sec")),
        P(("rad", "sec")),
        P(("rad", "sec")),
        P(("rad", "sec"), None),
    )
    return jax.shard_map(
        local,
        mesh=mesh,
        in_specs=placed,
        out_specs=(P(None, "rad", None, "sec"), P(None, ("rad", "sec"))),
        check_vma=False,
    )
```

profile of v0, /device:TPU:1, one launch (start us, length us, event | category | flops | bytes accessed | tf_op | source)
XLA Modules:
  0.0 208.0 jit_solution(9717823314005886017)
XLA Ops:
  0.7 1.1 fusion.24
  2.0 1.6 fusion.18
  3.9 3.5 %fusion.12 = f32[128,6,64]{0,2,1:T(8,128)S(1)} fusion(f32[4096,6]{0,1:T(8,128)S(1)} %maximum_bitcast_fusion, pred[4096,64]{0,1:T(8,128)(4,1)S(1)} %iota_compare_fusion.7, s32[4096]{0:T(1024)S(1)} %bitcast.91), kind=kOutput, calls=%fused_computation.13 | convolution fusion | flops 2418016256 | bytes 573440 | tf_op jit(solution)/shard_map/dot_general | solution.py:217
  7.7 0.9 reshape.194
  8.6 11.5 %all-to-all-start.2 = ((f32[128,1,384]{2,1,0:T(1,128)}), f32[128,1,384]{2,1,0:T(1,128)S(1)}, u32[]{:S(2)}, u32[]{:S(2)}) async-start(f32[128,1,384]{2,1,0:T(1,128)} %reshape.194), calls=%async_computation.2 | async-start | bytes 393216 | tf_op jit(solution)/shard_map/all_to_all | solution.py:220
  20.1 1.7 copy.36
  21.8 8.4 %all-to-all-done.2 = f32[128,1,384]{2,1,0:T(1,128)S(1)} async-done(((f32[128,1,384]{2,1,0:T(1,128)}), f32[128,1,384]{2,1,0:T(1,128)S(1)}, u32[]{:S(2)}, u32[]{:S(2)}) %all-to-all-start.2) | async-done | bytes 196640 | tf_op jit(solution)/shard_map/all_to_all | solution.py:220
  30.3 4.2 %all-to-all-start = ((f32[32,5,16,256]{3,2,1,0:T(8,128)}), f32[32,5,16,256]{3,2,1,0:T(8,128)S(1)}, u32[]{:S(2)}, u32[]{:S(2)}) async-start(f32[32,5,16,256]{3,2,1,0:T(8,128)} %bitcast.76), calls=%async_computation | async-start | bytes 5242880 | tf_op jit(solution)/shard_map/all_to_all | solution.py:179
  38.2 1.1 reduce.14
  40.5 1.1 slice.65
  41.6 27.3 %all-to-all-done = f32[32,5,16,256]{3,2,1,0:T(8,128)S(1)} async-done(((f32[32,5,16,256]{3,2,1,0:T(8,128)}), f32[32,5,16,256]{3,2,1,0:T(8,128)S(1)}, u32[]{:S(2)}, u32[]{:S(2)}) %all-to-all-start) | async-done | bytes 2621472 | tf_op jit(solution)/shard_map/all_to_all | solution.py:179
  68.9 1.5 copy-done.1
  70.4 7.0 %shard_map.86 = f32[32,1,80,256]{3,2,1,0:T(8,128)} custom-call(s32[1]{0:T(128)S(6)} %select_n.48.quotient_ref, s32[1]{0:T(128)S(6)} %select_n.49.remainder_ref, f32[32,1,80,256]{3,2,1,0:T(8,128)} %bitcast.81), custom_call_target="tpu_custom_call" | custom-call | tf_op jit(solution)/shard_map/pallas_call | solution.py:80
  77.4 6.5 %all-to-all-start.1 = ((f32[32,5,16,256]{3,2,1,0:T(8,128)}), f32[32,5,16,256]{3,2,1,0:T(8,128)}, u32[]{:S(2)}, u32[]{:S(2)}) async-start(f32[32,5,16,256]{3,2,1,0:T(8,128)} %bitcast.82), calls=%async_computation.1 | async-start | bytes 5242880 | tf_op jit(solution)/shard_map/all_to_all | solution.py:184
  84.5 4.2 %fusion.11 = f32[8192,256]{0,1:T(8,128)} fusion(s32[8192]{0:T(1024)S(1)} %get-tuple-element.19), kind=kLoop, calls=%fused_computation.12 | loop fusion | flops 4194304 | bytes 8421376 | tf_op jit(solution)/shard_map/convert_element_type | solution.py:235
  88.7 28.9 %all-to-all-done.1 = f32[32,5,16,256]{3,2,1,0:T(8,128)} async-done(((f32[32,5,16,256]{3,2,1,0:T(8,128)}), f32[32,5,16,256]{3,2,1,0:T(8,128)}, u32[]{:S(2)}, u32[]{:S(2)}) %all-to-all-start.1) | async-done | bytes 2621472 | tf_op jit(solution)/shard_map/all_to_all | solution.py:184
  117.6 2.1 copy.35
  119.7 1.4 slice_divide_fusion
  121.1 3.1 %copy.23 = f32[3,512,256]{1,2,0:T(8,128)} copy(f32[3,512,256]{2,1,0:T(8,128)} %bitcast.83) | data formatting | bytes 3145728 | tf_op jit(solution)/shard_map/reshape | solution.py:225
  124.2 17.0 %multiply_reduce_fusion = f32[8192,3]{0,1:T(4,128)S(1)} fusion(f32[8192,256]{0,1:T(8,128)} %fusion.11, f32[3,512,256]{1,2,0:T(8,128)} %copy.23, s32[8192]{0:T(1024)S(1)} %get-tuple-element.18), kind=kOutput, calls=%fused_computation.3 | convolution fusion | flops 19344105472 | bytes 10092544 | tf_op jit(solution)/shard_map/dot_general | solution.py:236
  141.9 18.3 %fusion = f32[512,3,256]{2,0,1:T(8,128)} fusion(f32[8192,3]{0,1:T(4,128)S(1)} %get-tuple-element.17, f32[8192,256]{0,1:T(8,128)} %fusion.11, s32[8192]{0:T(1024)S(1)} %get-tuple-element.18), kind=kOutput, calls=%fused_computation | convolution fusion | flops 19337838592 | bytes 10092544 | tf_op jit(solution)/shard_map/dot_general | solution.py:246
  160.2 1.8 slice_add_fusion
  163.4 1.9 fusion.44
  166.0 5.5 %collective-permute-start = (f32[7,2,16,256]{3,2,1,0:T(8,128)}, f32[7,2,16,256]{3,2,1,0:T(8,128)}, u32[]{:S(2)}, u32[]{:S(2)}) collective-permute-start(f32[7,2,16,256]{3,2,1,0:T(8,128)} %pad_maximum_fusion.2), channel_id=1, source_target_pairs={{0,32},{32,64},{64,96},{1,33},{33,65},{65,97},{2,34},{34,66},{66,9... | collective-permute-start | bytes 688136 | tf_op jit(solution)/shard_map/ppermute | solution.py:257
  171.5 0.7 pad_maximum_fusion.3
  172.2 1.9 collective-permute-start.1
  174.7 1.9 copy.27
  177.4 5.7 %collective-permute-start.3 = (f32[7,32,16,2]{1,2,3,0:T(8,128)S(1)}, f32[7,32,16,2]{1,2,3,0:T(8,128)S(1)}, u32[]{:S(2)}, u32[]{:S(2)}) collective-permute-start(f32[7,32,16,2]{1,2,3,0:T(8,128)S(1)} %pad_maximum_fusion.5), channel_id=1, source_target_pairs={{1,0},{2,1},{3,2},{4,3},{5,4},{6,5},{7,6},{8,7},{9,8},{10,9},{11,1... | collective-permute-start | bytes 86024 | tf_op jit(solution)/shard_map/ppermute | solution.py:272
  183.1 1.1 pad_maximum_fusion.1.s_ref
  184.9 2.0 copy.30.ah_ref
  186.9 2.0 copy.29.al_ref
  188.9 19.1 %shard_map.87 = f32[5,32,16,256]{3,2,1,0:T(8,128)} custom-call(f32[5,32,16,256]{3,2,1,0:T(8,128)} %copy-done, f32[2,32,16,256]{3,2,1,0:T(8,128)} %pad_maximum_fusion.1.s_ref, f32[7,2,16,256]{3,2,1,0:T(8,128)} %collective-permute-done.rl_ref, f32[7,2,16,256]{3,2,1,0:T(8,128)} %collective-permute-done.1.rh_ref, f32[7,32,16,2]{3,2,1,0:T(8,128)} %copy.29.al_ref, ...), custom_call_target="tpu_custom_call" | custom-call | tf_op jit(solution)/shard_map/pallas_call | solution.py:157
  (57 shorter events, 8.4 us)
Async XLA Ops:
  0.6 3.2 %copy-start.6 = (s32[4096,1]{0,1:T(1,128)S(1)}, s32[4096,1]{0,1:T(1,128)}, u32[]{:S(2)}) copy-start(s32[4096,1]{0,1:T(1,128)} %param.13) | copy-start | bytes 49156
  0.6 3.0 %copy-start.7 = (s32[4096]{0:T(1024)S(1)}, s32[4096]{0:T(1024)}, u32[]{:S(2)}) copy-start(s32[4096]{0:T(1024)} %param.12) | copy-start | bytes 49156
  0.7 3.1 %copy-start.8 = (f32[4096]{0:T(1024)S(1)}, f32[4096]{0:T(1024)}, u32[]{:S(2)}) copy-start(f32[4096]{0:T(1024)} %param.11) | copy-start | bytes 49156
  0.7 3.1 %copy-start.9 = (f32[4096]{0:T(1024)S(1)}, f32[4096]{0:T(1024)}, u32[]{:S(2)}) copy-start(f32[4096]{0:T(1024)} %param.10) | copy-start | bytes 49156
  0.7 3.1 %copy-start.5 = (f32[3,4096]{1,0:T(4,128)S(1)}, f32[3,4096]{1,0:T(4,128)}, u32[]{:S(2)}) copy-start(f32[3,4096]{1,0:T(4,128)} %param.9) | copy-start | bytes 147460
  3.9 16.2 %copy-start.4 = (f32[5,32,16,256]{3,2,1,0:T(8,128)S(1)}, f32[5,32,16,256]{3,2,1,0:T(8,128)}, u32[]{:S(2)}) copy-start(f32[5,32,16,256]{3,2,1,0:T(8,128)} %param.7) | copy-start | bytes 7864324
  8.6 21.7 %all-to-all-start.2 = ((f32[128,1,384]{2,1,0:T(1,128)}), f32[128,1,384]{2,1,0:T(1,128)S(1)}, u32[]{:S(2)}, u32[]{:S(2)}) async-start(f32[128,1,384]{2,1,0:T(1,128)} %reshape.194), calls=%async_computation.2 | async-start | bytes 393216 | tf_op jit(solution)/shard_map/all_to_all | solution.py:220
  30.3 4.2 %copy-start.10 = (s32[32]{0:T(128)S(1)}, s32[32]{0:T(128)}, u32[]{:S(2)}) copy-start(s32[32]{0:T(128)} %param.8) | copy-start | bytes 388
  30.3 38.6 %all-to-all-start = ((f32[32,5,16,256]{3,2,1,0:T(8,128)}), f32[32,5,16,256]{3,2,1,0:T(8,128)S(1)}, u32[]{:S(2)}, u32[]{:S(2)}) async-start(f32[32,5,16,256]{3,2,1,0:T(8,128)} %bitcast.76), calls=%async_computation | async-start | bytes 5242880 | tf_op jit(solution)/shard_map/all_to_all | solution.py:179
  68.9 1.5 copy-start.1
  77.4 40.2 %all-to-all-start.1 = ((f32[32,5,16,256]{3,2,1,0:T(8,128)}), f32[32,5,16,256]{3,2,1,0:T(8,128)}, u32[]{:S(2)}, u32[]{:S(2)}) async-start(f32[32,5,16,256]{3,2,1,0:T(8,128)} %bitcast.82), calls=%async_computation.1 | async-start | bytes 5242880 | tf_op jit(solution)/shard_map/all_to_all | solution.py:184
  162.2 0.8 copy-start.2
  163.4 1.9 copy-start
  165.3 17.8 %copy-start.3 = (f32[1,32,16,256]{3,2,1,0:T(8,128)S(1)}, f32[1,32,16,256]{3,2,1,0:T(8,128)}, u32[]{:S(2)}) copy-start(f32[1,32,16,256]{3,2,1,0:T(8,128)} %copy-done.2) | copy-start | bytes 1572868
  166.0 22.9 %collective-permute-start = (f32[7,2,16,256]{3,2,1,0:T(8,128)}, f32[7,2,16,256]{3,2,1,0:T(8,128)}, u32[]{:S(2)}, u32[]{:S(2)}) collective-permute-start(f32[7,2,16,256]{3,2,1,0:T(8,128)} %pad_maximum_fusion.2), channel_id=1, source_target_pairs={{0,32},{32,64},{64,96},{1,33},{33,65},{65,97},{2,34},{34,66},{66,9... | collective-permute-start | bytes 688136 | tf_op jit(solution)/shard_map/ppermute | solution.py:257
  172.2 16.7 %collective-permute-start.1 = (f32[7,2,16,256]{3,2,1,0:T(8,128)}, f32[7,2,16,256]{3,2,1,0:T(8,128)}, u32[]{:S(2)}, u32[]{:S(2)}) collective-permute-start(f32[7,2,16,256]{3,2,1,0:T(8,128)} %pad_maximum_fusion.3), channel_id=1, source_target_pairs={{32,0},{64,32},{96,64},{33,1},{65,33},{97,65},{34,2},{66,34},{98,6... | collective-permute-start | bytes 688136 | tf_op jit(solution)/shard_map/ppermute | solution.py:262
  177.3 9.6 %collective-permute-start.2 = (f32[7,32,16,2]{1,2,3,0:T(8,128)S(1)}, f32[7,32,16,2]{1,2,3,0:T(8,128)S(1)}, u32[]{:S(2)}, u32[]{:S(2)}) collective-permute-start(f32[7,32,16,2]{1,2,3,0:T(8,128)S(1)} %pad_maximum_fusion.4), channel_id=1, source_target_pairs={{0,1},{1,2},{2,3},{3,4},{4,5},{5,6},{6,7},{7,8},{8,9},{9,10},{10,1... | collective-permute-start | bytes 86024 | tf_op jit(solution)/shard_map/ppermute | solution.py:267
  177.4 7.5 %collective-permute-start.3 = (f32[7,32,16,2]{1,2,3,0:T(8,128)S(1)}, f32[7,32,16,2]{1,2,3,0:T(8,128)S(1)}, u32[]{:S(2)}, u32[]{:S(2)}) collective-permute-start(f32[7,32,16,2]{1,2,3,0:T(8,128)S(1)} %pad_maximum_fusion.5), channel_id=1, source_target_pairs={{1,0},{2,1},{3,2},{4,3},{5,4},{6,5},{7,6},{8,7},{9,8},{10,9},{11,1... | collective-permute-start | bytes 86024 | tf_op jit(solution)/shard_map/ppermute | solution.py:272
where the time goes:
time: 209 us; the launch traced here: 208 us
  waiting for transfers between devices  65.4 us (31%)
  matrix products  40.6 us (19%)
  starting transfers between devices  35.3 us (17%)
  Pallas kernels  26.1 us (12%)
  local copies, waits for them, and re-layouts  22.8 us (11%)
  other arithmetic  14.2 us (7%)
  between operations  3.61 us (2%)
    all_to_all x1, waiting for transfers between devices, local(): lax.all_to_all(rolled, 'sec', split_axis=0, concat_axis=0, tiled=True)  28.9 us
    all_to_all x1, waiting for transfers between devices, local(): lax.all_to_all(by_radius, 'sec', split_axis=0, concat_axis=0, tiled=True)  27.3 us
    pallas_call x1, Pallas kernels, transport(): pl.pallas_call(kernel, out_shape=jax.ShapeDtypeStruct(dragged.shape, drag...  19.1 us
    dot_general x1, matrix products, local(): jnp.dot(row_hot.T, spread, precision=lax.Precision.HIGH, preferred_elemen...  18.3 us
    dot_general x1, matrix products, local(): jnp.dot(row_hot, velocity_rows, precision=lax.Precision.HIGH, preferred_e...  17 us
    all_to_all x1, starting transfers between devices, local(): lax.all_to_all(outbox, ('rad', 'sec'), split_axis=0, concat_axis=0, tiled...  11.5 us
    all_to_all x1, waiting for transfers between devices, local(): lax.all_to_all(outbox, ('rad', 'sec'), split_axis=0, concat_axis=0, tiled...  8.44 us
    pallas_call x1, Pallas kernels, sector_roll(): pl.pallas_call(kernel, out_shape=jax.ShapeDtypeStruct(ring.shape, ring.dt...  7 us
  transfers between devices with their start and end apart: 7, of which 4 were waited for; matrix products, arithmetic and copies ran while one was open for 10% of the time, Pallas kernels for 0%

commit v1 on v0

--- a/solution.py
+++ b/solution.py
@@ -113,7 +113,7 @@
 
         def radial_at(f, r, offset):
             k = r + offset
-            inner = d_ref[f, jnp.clip(k, 0, radii - 1)] if f < fields else s_ref[0, jnp.clip(k, 0, radii - 1)]
+            inner = d_ref[f, jnp.clip(k, 0, radii - 1)]
             low = rl_ref[f, jnp.clip(k + 2, 0, 1)]
             high = rh_ref[f, jnp.clip(k - radii, 0, 1)]
             return jnp.where(k < 0, low, jnp.where(k >= radii, high, inner))
@@ -131,27 +131,45 @@
                     moved = jnp.where(lane == cells - offset + j, edge, moved)
             return moved
 
-        def body(r, carry):
-            sr = s_ref[0, r]
-            sa = s_ref[1, r]
-            sr_m1 = radial_at(fields, r, -1)
-            sr_p1 = radial_at(fields, r, 1)
-            sa_m1 = ring_at(sa, fields + 1, r, -1)
-            sa_p1 = ring_at(sa, fields + 1, r, 1)
-            for f in range(fields):
-                v0 = d_ref[f, r]
-                radial = face_divergence(
-                    radial_at(f, r, -2), radial_at(f, r, -1), v0, radial_at(f, r, 1), radial_at(f, r, 2),
-                    sr_m1, sr, sr_p1,
+        def speed_at(r, offset):
+            k = r + offset
+            inner = s_ref[0, jnp.clip(k, 0, radii - 1)]
+            low = rl_ref[fields, jnp.clip(k + 2, 0, 1)]
+            high = rh_ref[fields, jnp.clip(k - radii, 0, 1)]
+            return jnp.where(k < 0, low, jnp.where(k >= radii, high, inner))
+
+        def flux(left, right, w):
+            return w * 0.5 * (left + right) - 0.5 * (jnp.abs(w) + 1.0) * (right - left)
+
+        def field_pass(f, unused):
+            v_m2 = radial_at(f, 0, -2)
+            v_m1 = radial_at(f, 0, -1)
+            v_0 = d_ref[f, 0]
+            v_p1 = radial_at(f, 0, 1)
+            s_m1 = speed_at(0, -1)
+            s_0 = s_ref[0, 0]
+            slope_m1 = minmod(v_m1 - v_m2, v_0 - v_m1)
+            slope_0 = minmod(v_0 - v_m1, v_p1 - v_0)
+            start = (v_0, v_p1, slope_0, flux(v_m1 + 0.5 * slope_m1, v_0 - 0.5 * slope_0, 0.5 * (s_m1 + s_0)), s_0)
+
+            def body(r, carry):
+                v_r, v_r1, slope_r, lower, s_r = carry
+                v_r2 = radial_at(f, r, 2)
+                s_r1 = speed_at(r, 1)
+                slope_r1 = minmod(v_r1 - v_r, v_r2 - v_r1)
+                upper = flux(v_r + 0.5 * slope_r, v_r1 - 0.5 * slope_r1, 0.5 * (s_r + s_r1))
+                sa = s_ref[1, r]
+                azimuthal = face_divergence(
+                    ring_at(v_r, f, r, -2), ring_at(v_r, f, r, -1), v_r, ring_at(v_r, f, r, 1), ring_at(v_r, f, r, 2),
+                    ring_at(sa, fields + 1, r, -1), sa, ring_at(sa, fields + 1, r, 1),
                 )
-                azimuthal = face_divergence(
-                    ring_at(v0, f, r, -2), ring_at(v0, f, r, -1), v0, ring_at(v0, f, r, 1), ring_at(v0, f, r, 2),
-                    sa_m1, sa, sa_p1,
-                )
-                out_ref[f, r] = v0 - rate_r * radial - rate_a * azimuthal
-            return carry
-
-        lax.fori_loop(0, radii, body, 0)
+                out_ref[f, r] = v_r - rate_r * (upper - lower) - rate_a * azimuthal
+                return (v_r1, v_r2, slope_r1, upper, s_r1)
+
+            lax.fori_loop(0, radii, body, start)
+            return unused
+
+        lax.fori_loop(0, fields, field_pass, 0)
 
     vmem = pl.BlockSpec(memory_space=pltpu.VMEM)
     return pl.pallas_call(

time: 209 us -> 215 us (1.029)
  Pallas kernels: 26.1 us -> 32.6 us
    pallas_call x1, Pallas kernels: 19.1 us -> 25.6 us  [transport(): pl.pallas_call(kernel, out_shape=jax.ShapeDtypeStruct(dragged.shape, drag...]
  transfers between devices with their start and end apart: 7 -> 7, of which waited for: 4 -> 4; matrix products, arithmetic and copies ran while one was open for 10% -> 9% of each run, Pallas kernels for 0% -> 0%
where the time goes in v1:
time: 215 us; the launch traced here: 214 us
  waiting for transfers between devices  65.4 us (30%)
  matrix products  40.6 us (19%)
  starting transfers between devices  35.3 us (16%)
  Pallas kernels  32.6 us (15%)
  local copies, waits for them, and re-layouts  22.8 us (11%)
  other arithmetic  14.2 us (7%)
  between operations  3.61 us (2%)
    all_to_all x1, waiting for transfers between devices, local(): lax.all_to_all(rolled, 'sec', split_axis=0, concat_axis=0, tiled=True)  28.9 us
    all_to_all x1, waiting for transfers between devices, local(): lax.all_to_all(by_radius, 'sec', split_axis=0, concat_axis=0, tiled=True)  27.3 us
    pallas_call x1, Pallas kernels, transport(): pl.pallas_call(kernel, out_shape=jax.ShapeDtypeStruct(dragged.shape, drag...  25.6 us
    dot_general x1, matrix products, local(): jnp.dot(row_hot.T, spread, precision=lax.Precision.HIGH, preferred_elemen...  18.3 us
    dot_general x1, matrix products, local(): jnp.dot(row_hot, velocity_rows, precision=lax.Precision.HIGH, preferred_e...  17 us
    all_to_all x1, starting transfers between devices, local(): lax.all_to_all(outbox, ('rad', 'sec'), split_axis=0, concat_axis=0, tiled...  11.5 us
    all_to_all x1, waiting for transfers between devices, local(): lax.all_to_all(outbox, ('rad', 'sec'), split_axis=0, concat_axis=0, tiled...  8.44 us
    pallas_call x1, Pallas kernels, sector_roll(): pl.pallas_call(kernel, out_shape=jax.ShapeDtypeStruct(ring.shape, ring.dt...  7 us
  transfers between devices with their start and end apart: 7, of which 4 were waited for; matrix products, arithmetic and copies ran while one was open for 9% of the time, Pallas kernels for 0%

profile of v1, /device:TPU:1, one launch (start us, length us, event | category | flops | bytes accessed | tf_op | source)
XLA Modules:
  0.0 214.5 jit_solution(1769685442262334789)
XLA Ops:
  0.7 1.1 fusion.24
  2.0 1.6 fusion.18
  3.9 3.5 %fusion.12 = f32[128,6,64]{0,2,1:T(8,128)S(1)} fusion(f32[4096,6]{0,1:T(8,128)S(1)} %maximum_bitcast_fusion, pred[4096,64]{0,1:T(8,128)(4,1)S(1)} %iota_compare_fusion.7, s32[4096]{0:T(1024)S(1)} %bitcast.91), kind=kOutput, calls=%fused_computation.13 | convolution fusion | flops 2418016256 | bytes 573440 | tf_op jit(solution)/shard_map/dot_general | solution.py:235
  7.7 0.9 reshape.194
  8.6 11.5 %all-to-all-start.2 = ((f32[128,1,384]{2,1,0:T(1,128)}), f32[128,1,384]{2,1,0:T(1,128)S(1)}, u32[]{:S(2)}, u32[]{:S(2)}) async-start(f32[128,1,384]{2,1,0:T(1,128)} %reshape.194), calls=%async_computation.2 | async-start | bytes 393216 | tf_op jit(solution)/shard_map/all_to_all | solution.py:238
  20.1 1.7 copy.36
  21.8 8.4 %all-to-all-done.2 = f32[128,1,384]{2,1,0:T(1,128)S(1)} async-done(((f32[128,1,384]{2,1,0:T(1,128)}), f32[128,1,384]{2,1,0:T(1,128)S(1)}, u32[]{:S(2)}, u32[]{:S(2)}) %all-to-all-start.2) | async-done | bytes 196640 | tf_op jit(solution)/shard_map/all_to_all | solution.py:238
  30.3 4.2 %all-to-all-start = ((f32[32,5,16,256]{3,2,1,0:T(8,128)}), f32[32,5,16,256]{3,2,1,0:T(8,128)S(1)}, u32[]{:S(2)}, u32[]{:S(2)}) async-start(f32[32,5,16,256]{3,2,1,0:T(8,128)} %bitcast.76), calls=%async_computation | async-start | bytes 5242880 | tf_op jit(solution)/shard_map/all_to_all | solution.py:197
  38.2 1.1 reduce.14
  40.5 1.1 slice.65
  41.6 27.3 %all-to-all-done = f32[32,5,16,256]{3,2,1,0:T(8,128)S(1)} async-done(((f32[32,5,16,256]{3,2,1,0:T(8,128)}), f32[32,5,16,256]{3,2,1,0:T(8,128)S(1)}, u32[]{:S(2)}, u32[]{:S(2)}) %all-to-all-start) | async-done | bytes 2621472 | tf_op jit(solution)/shard_map/all_to_all | solution.py:197
  68.9 1.5 copy-done.1
  70.4 7.0 %shard_map.86 = f32[32,1,80,256]{3,2,1,0:T(8,128)} custom-call(s32[1]{0:T(128)S(6)} %select_n.48.quotient_ref, s32[1]{0:T(128)S(6)} %select_n.49.remainder_ref, f32[32,1,80,256]{3,2,1,0:T(8,128)} %bitcast.81), custom_call_target="tpu_custom_call" | custom-call | tf_op jit(solution)/shard_map/pallas_call | solution.py:80
  77.4 6.5 %all-to-all-start.1 = ((f32[32,5,16,256]{3,2,1,0:T(8,128)}), f32[32,5,16,256]{3,2,1,0:T(8,128)}, u32[]{:S(2)}, u32[]{:S(2)}) async-start(f32[32,5,16,256]{3,2,1,0:T(8,128)} %bitcast.82), calls=%async_computation.1 | async-start | bytes 5242880 | tf_op jit(solution)/shard_map/all_to_all | solution.py:202
  84.5 4.2 %fusion.11 = f32[8192,256]{0,1:T(8,128)} fusion(s32[8192]{0:T(1024)S(1)} %get-tuple-element.19), kind=kLoop, calls=%fused_computation.12 | loop fusion | flops 4194304 | bytes 8421376 | tf_op jit(solution)/shard_map/convert_element_type | solution.py:253
  88.7 28.9 %all-to-all-done.1 = f32[32,5,16,256]{3,2,1,0:T(8,128)} async-done(((f32[32,5,16,256]{3,2,1,0:T(8,128)}), f32[32,5,16,256]{3,2,1,0:T(8,128)}, u32[]{:S(2)}, u32[]{:S(2)}) %all-to-all-start.1) | async-done | bytes 2621472 | tf_op jit(solution)/shard_map/all_to_all | solution.py:202
  117.6 2.1 copy.35
  119.7 1.4 slice_divide_fusion
  121.1 3.1 %copy.23 = f32[3,512,256]{1,2,0:T(8,128)} copy(f32[3,512,256]{2,1,0:T(8,128)} %bitcast.83) | data formatting | bytes 3145728 | tf_op jit(solution)/shard_map/reshape | solution.py:243
  124.2 17.0 %multiply_reduce_fusion = f32[8192,3]{0,1:T(4,128)S(1)} fusion(f32[8192,256]{0,1:T(8,128)} %fusion.11, f32[3,512,256]{1,2,0:T(8,128)} %copy.23, s32[8192]{0:T(1024)S(1)} %get-tuple-element.18), kind=kOutput, calls=%fused_computation.3 | convolution fusion | flops 19344105472 | bytes 10092544 | tf_op jit(solution)/shard_map/dot_general | solution.py:254
  141.9 18.3 %fusion = f32[512,3,256]{2,0,1:T(8,128)} fusion(f32[8192,3]{0,1:T(4,128)S(1)} %get-tuple-element.17, f32[8192,256]{0,1:T(8,128)} %fusion.11, s32[8192]{0:T(1024)S(1)} %get-tuple-element.18), kind=kOutput, calls=%fused_computation | convolution fusion | flops 19337838592 | bytes 10092544 | tf_op jit(solution)/shard_map/dot_general | solution.py:264
  160.2 1.8 slice_add_fusion
  163.4 1.9 fusion.44
  166.0 5.5 %collective-permute-start = (f32[7,2,16,256]{3,2,1,0:T(8,128)}, f32[7,2,16,256]{3,2,1,0:T(8,128)}, u32[]{:S(2)}, u32[]{:S(2)}) collective-permute-start(f32[7,2,16,256]{3,2,1,0:T(8,128)} %pad_maximum_fusion.2), channel_id=1, source_target_pairs={{0,32},{32,64},{64,96},{1,33},{33,65},{65,97},{2,34},{34,66},{66,9... | collective-permute-start | bytes 688136 | tf_op jit(solution)/shard_map/ppermute | solution.py:275
  171.5 0.7 pad_maximum_fusion.3
  172.2 1.9 collective-permute-start.1
  174.7 1.9 copy.27
  177.4 5.7 %collective-permute-start.3 = (f32[7,32,16,2]{1,2,3,0:T(8,128)S(1)}, f32[7,32,16,2]{1,2,3,0:T(8,128)S(1)}, u32[]{:S(2)}, u32[]{:S(2)}) collective-permute-start(f32[7,32,16,2]{1,2,3,0:T(8,128)S(1)} %pad_maximum_fusion.5), channel_id=1, source_target_pairs={{1,0},{2,1},{3,2},{4,3},{5,4},{6,5},{7,6},{8,7},{9,8},{10,9},{11,1... | collective-permute-start | bytes 86024 | tf_op jit(solution)/shard_map/ppermute | solution.py:290
  183.1 1.1 pad_maximum_fusion.1.s_ref
  184.9 2.0 copy.30.ah_ref
  186.9 2.0 copy.29.al_ref
  188.9 25.6 %shard_map.87 = f32[5,32,16,256]{3,2,1,0:T(8,128)} custom-call(f32[5,32,16,256]{3,2,1,0:T(8,128)} %copy-done, f32[2,32,16,256]{3,2,1,0:T(8,128)} %pad_maximum_fusion.1.s_ref, f32[7,2,16,256]{3,2,1,0:T(8,128)} %collective-permute-done.rl_ref, f32[7,2,16,256]{3,2,1,0:T(8,128)} %collective-permute-done.1.rh_ref, f32[7,32,16,2]{3,2,1,0:T(8,128)} %copy.29.al_ref, ...), custom_call_target="tpu_custom_call" | custom-call | tf_op jit(solution)/shard_map/pallas_call | solution.py:175
  (57 shorter events, 8.4 us)
Async XLA Ops:
  0.6 3.2 %copy-start.6 = (s32[4096,1]{0,1:T(1,128)S(1)}, s32[4096,1]{0,1:T(1,128)}, u32[]{:S(2)}) copy-start(s32[4096,1]{0,1:T(1,128)} %param.13) | copy-start | bytes 49156
  0.6 3.0 %copy-start.7 = (s32[4096]{0:T(1024)S(1)}, s32[4096]{0:T(1024)}, u32[]{:S(2)}) copy-start(s32[4096]{0:T(1024)} %param.12) | copy-start | bytes 49156
  0.7 3.1 %copy-start.8 = (f32[4096]{0:T(1024)S(1)}, f32[4096]{0:T(1024)}, u32[]{:S(2)}) copy-start(f32[4096]{0:T(1024)} %param.11) | copy-start | bytes 49156
  0.7 3.1 %copy-start.9 = (f32[4096]{0:T(1024)S(1)}, f32[4096]{0:T(1024)}, u32[]{:S(2)}) copy-start(f32[4096]{0:T(1024)} %param.10) | copy-start | bytes 49156
  0.7 3.1 %copy-start.5 = (f32[3,4096]{1,0:T(4,128)S(1)}, f32[3,4096]{1,0:T(4,128)}, u32[]{:S(2)}) copy-start(f32[3,4096]{1,0:T(4,128)} %param.9) | copy-start | bytes 147460
  3.9 16.2 %copy-start.4 = (f32[5,32,16,256]{3,2,1,0:T(8,128)S(1)}, f32[5,32,16,256]{3,2,1,0:T(8,128)}, u32[]{:S(2)}) copy-start(f32[5,32,16,256]{3,2,1,0:T(8,128)} %param.7) | copy-start | bytes 7864324
  8.6 21.7 %all-to-all-start.2 = ((f32[128,1,384]{2,1,0:T(1,128)}), f32[128,1,384]{2,1,0:T(1,128)S(1)}, u32[]{:S(2)}, u32[]{:S(2)}) async-start(f32[128,1,384]{2,1,0:T(1,128)} %reshape.194), calls=%async_computation.2 | async-start | bytes 393216 | tf_op jit(solution)/shard_map/all_to_all | solution.py:238
  30.3 4.2 %copy-start.10 = (s32[32]{0:T(128)S(1)}, s32[32]{0:T(128)}, u32[]{:S(2)}) copy-start(s32[32]{0:T(128)} %param.8) | copy-start | bytes 388
  30.3 38.6 %all-to-all-start = ((f32[32,5,16,256]{3,2,1,0:T(8,128)}), f32[32,5,16,256]{3,2,1,0:T(8,128)S(1)}, u32[]{:S(2)}, u32[]{:S(2)}) async-start(f32[32,5,16,256]{3,2,1,0:T(8,128)} %bitcast.76), calls=%async_computation | async-start | bytes 5242880 | tf_op jit(solution)/shard_map/all_to_all | solution.py:197
  68.9 1.5 copy-start.1
  77.4 40.2 %all-to-all-start.1 = ((f32[32,5,16,256]{3,2,1,0:T(8,128)}), f32[32,5,16,256]{3,2,1,0:T(8,128)}, u32[]{:S(2)}, u32[]{:S(2)}) async-start(f32[32,5,16,256]{3,2,1,0:T(8,128)} %bitcast.82), calls=%async_computation.1 | async-start | bytes 5242880 | tf_op jit(solution)/shard_map/all_to_all | solution.py:202
  162.2 0.8 copy-start.2
  163.4 1.9 copy-start
  165.3 17.8 %copy-start.3 = (f32[1,32,16,256]{3,2,1,0:T(8,128)S(1)}, f32[1,32,16,256]{3,2,1,0:T(8,128)}, u32[]{:S(2)}) copy-start(f32[1,32,16,256]{3,2,1,0:T(8,128)} %copy-done.2) | copy-start | bytes 1572868
  166.0 22.9 %collective-permute-start = (f32[7,2,16,256]{3,2,1,0:T(8,128)}, f32[7,2,16,256]{3,2,1,0:T(8,128)}, u32[]{:S(2)}, u32[]{:S(2)}) collective-permute-start(f32[7,2,16,256]{3,2,1,0:T(8,128)} %pad_maximum_fusion.2), channel_id=1, source_target_pairs={{0,32},{32,64},{64,96},{1,33},{33,65},{65,97},{2,34},{34,66},{66,9... | collective-permute-start | bytes 688136 | tf_op jit(solution)/shard_map/ppermute | solution.py:275
  172.2 16.7 %collective-permute-start.1 = (f32[7,2,16,256]{3,2,1,0:T(8,128)}, f32[7,2,16,256]{3,2,1,0:T(8,128)}, u32[]{:S(2)}, u32[]{:S(2)}) collective-permute-start(f32[7,2,16,256]{3,2,1,0:T(8,128)} %pad_maximum_fusion.3), channel_id=1, source_target_pairs={{32,0},{64,32},{96,64},{33,1},{65,33},{97,65},{34,2},{66,34},{98,6... | collective-permute-start | bytes 688136 | tf_op jit(solution)/shard_map/ppermute | solution.py:280
  177.3 9.6 %collective-permute-start.2 = (f32[7,32,16,2]{1,2,3,0:T(8,128)S(1)}, f32[7,32,16,2]{1,2,3,0:T(8,128)S(1)}, u32[]{:S(2)}, u32[]{:S(2)}) collective-permute-start(f32[7,32,16,2]{1,2,3,0:T(8,128)S(1)} %pad_maximum_fusion.4), channel_id=1, source_target_pairs={{0,1},{1,2},{2,3},{3,4},{4,5},{5,6},{6,7},{7,8},{8,9},{9,10},{10,1... | collective-permute-start | bytes 86024 | tf_op jit(solution)/shard_map/ppermute | solution.py:285
  177.4 7.5 %collective-permute-start.3 = (f32[7,32,16,2]{1,2,3,0:T(8,128)S(1)}, f32[7,32,16,2]{1,2,3,0:T(8,128)S(1)}, u32[]{:S(2)}, u32[]{:S(2)}) collective-permute-start(f32[7,32,16,2]{1,2,3,0:T(8,128)S(1)} %pad_maximum_fusion.5), channel_id=1, source_target_pairs={{1,0},{2,1},{3,2},{4,3},{5,4},{6,5},{7,6},{8,7},{9,8},{10,9},{11,1... | collective-permute-start | bytes 86024 | tf_op jit(solution)/shard_map/ppermute | solution.py:290

commit v2 on v0

--- a/solution.py
+++ b/solution.py
@@ -89,11 +89,8 @@
     )(quotient, remainder, ring)
 
 
-def sign_of(x):
-    return jnp.where(x > 0, 1.0, jnp.where(x < 0, -1.0, 0.0))
-
 def minmod(a, b):
-    return 0.5 * (sign_of(a) + sign_of(b)) * jnp.minimum(jnp.abs(a), jnp.abs(b))
+    return jnp.maximum(jnp.minimum(a, b), 0.0) + jnp.minimum(jnp.maximum(a, b), 0.0)
 
 def face_divergence(v_m2, v_m1, v0, v_p1, v_p2, s_m1, s0, s_p1):
     slope_m1 = minmod(v_m1 - v_m2, v0 - v_m1)

time: 209 us -> 206 us (0.986)
  Pallas kernels: 26.1 us -> 23 us
    pallas_call x1, Pallas kernels: 19.1 us -> 16 us  [transport(): pl.pallas_call(kernel, out_shape=jax.ShapeDtypeStruct(dragged.shape, drag...]
where the time goes in v2:
time: 206 us; the launch traced here: 205 us
  waiting for transfers between devices  65.4 us (32%)
  matrix products  40.6 us (20%)
  starting transfers between devices  35.3 us (17%)
  Pallas kernels  23 us (11%)
  local copies, waits for them, and re-layouts  22.8 us (11%)
  other arithmetic  14.2 us (7%)
  between operations  3.61 us (2%)
    all_to_all x1, waiting for transfers between devices, local(): lax.all_to_all(rolled, 'sec', split_axis=0, concat_axis=0, tiled=True)  28.9 us
    all_to_all x1, waiting for transfers between devices, local(): lax.all_to_all(by_radius, 'sec', split_axis=0, concat_axis=0, tiled=True)  27.3 us
    dot_general x1, matrix products, local(): jnp.dot(row_hot.T, spread, precision=lax.Precision.HIGH, preferred_elemen...  18.3 us
    dot_general x1, matrix products, local(): jnp.dot(row_hot, velocity_rows, precision=lax.Precision.HIGH, preferred_e...  17 us
    pallas_call x1, Pallas kernels, transport(): pl.pallas_call(kernel, out_shape=jax.ShapeDtypeStruct(dragged.shape, drag...  16 us
    all_to_all x1, starting transfers between devices, local(): lax.all_to_all(outbox, ('rad', 'sec'), split_axis=0, concat_axis=0, tiled...  11.5 us
    all_to_all x1, waiting for transfers between devices, local(): lax.all_to_all(outbox, ('rad', 'sec'), split_axis=0, concat_axis=0, tiled...  8.44 us
    pallas_call x1, Pallas kernels, sector_roll(): pl.pallas_call(kernel, out_shape=jax.ShapeDtypeStruct(ring.shape, ring.dt...  7 us
  transfers between devices with their start and end apart: 7, of which 4 were waited for; matrix products, arithmetic and copies ran while one was open for 10% of the time, Pallas kernels for 0%

profile of v2, /device:TPU:1, one launch (start us, length us, event | category | flops | bytes accessed | tf_op | source)
XLA Modules:
  0.0 204.9 jit_solution(8722446609301300941)
XLA Ops:
  0.7 1.1 fusion.24
  2.0 1.6 fusion.18
  3.9 3.5 %fusion.12 = f32[128,6,64]{0,2,1:T(8,128)S(1)} fusion(f32[4096,6]{0,1:T(8,128)S(1)} %maximum_bitcast_fusion, pred[4096,64]{0,1:T(8,128)(4,1)S(1)} %iota_compare_fusion.7, s32[4096]{0:T(1024)S(1)} %bitcast.91), kind=kOutput, calls=%fused_computation.13 | convolution fusion | flops 2418016256 | bytes 573440 | tf_op jit(solution)/shard_map/dot_general | solution.py:214
  7.7 0.9 reshape.194
  8.6 11.5 %all-to-all-start.2 = ((f32[128,1,384]{2,1,0:T(1,128)}), f32[128,1,384]{2,1,0:T(1,128)S(1)}, u32[]{:S(2)}, u32[]{:S(2)}) async-start(f32[128,1,384]{2,1,0:T(1,128)} %reshape.194), calls=%async_computation.2 | async-start | bytes 393216 | tf_op jit(solution)/shard_map/all_to_all | solution.py:217
  20.1 1.7 copy.36
  21.8 8.4 %all-to-all-done.2 = f32[128,1,384]{2,1,0:T(1,128)S(1)} async-done(((f32[128,1,384]{2,1,0:T(1,128)}), f32[128,1,384]{2,1,0:T(1,128)S(1)}, u32[]{:S(2)}, u32[]{:S(2)}) %all-to-all-start.2) | async-done | bytes 196640 | tf_op jit(solution)/shard_map/all_to_all | solution.py:217
  30.3 4.2 %all-to-all-start = ((f32[32,5,16,256]{3,2,1,0:T(8,128)}), f32[32,5,16,256]{3,2,1,0:T(8,128)S(1)}, u32[]{:S(2)}, u32[]{:S(2)}) async-start(f32[32,5,16,256]{3,2,1,0:T(8,128)} %bitcast.76), calls=%async_computation | async-start | bytes 5242880 | tf_op jit(solution)/shard_map/all_to_all | solution.py:176
  38.2 1.1 reduce.14
  40.5 1.1 slice.65
  41.6 27.3 %all-to-all-done = f32[32,5,16,256]{3,2,1,0:T(8,128)S(1)} async-done(((f32[32,5,16,256]{3,2,1,0:T(8,128)}), f32[32,5,16,256]{3,2,1,0:T(8,128)S(1)}, u32[]{:S(2)}, u32[]{:S(2)}) %all-to-all-start) | async-done | bytes 2621472 | tf_op jit(solution)/shard_map/all_to_all | solution.py:176
  68.9 1.5 copy-done.1
  70.4 7.0 %shard_map.86 = f32[32,1,80,256]{3,2,1,0:T(8,128)} custom-call(s32[1]{0:T(128)S(6)} %select_n.48.quotient_ref, s32[1]{0:T(128)S(6)} %select_n.49.remainder_ref, f32[32,1,80,256]{3,2,1,0:T(8,128)} %bitcast.81), custom_call_target="tpu_custom_call" | custom-call | tf_op jit(solution)/shard_map/pallas_call | solution.py:80
  77.4 6.5 %all-to-all-start.1 = ((f32[32,5,16,256]{3,2,1,0:T(8,128)}), f32[32,5,16,256]{3,2,1,0:T(8,128)}, u32[]{:S(2)}, u32[]{:S(2)}) async-start(f32[32,5,16,256]{3,2,1,0:T(8,128)} %bitcast.82), calls=%async_computation.1 | async-start | bytes 5242880 | tf_op jit(solution)/shard_map/all_to_all | solution.py:181
  84.5 4.2 %fusion.11 = f32[8192,256]{0,1:T(8,128)} fusion(s32[8192]{0:T(1024)S(1)} %get-tuple-element.19), kind=kLoop, calls=%fused_computation.12 | loop fusion | flops 4194304 | bytes 8421376 | tf_op jit(solution)/shard_map/convert_element_type | solution.py:232
  88.7 28.9 %all-to-all-done.1 = f32[32,5,16,256]{3,2,1,0:T(8,128)} async-done(((f32[32,5,16,256]{3,2,1,0:T(8,128)}), f32[32,5,16,256]{3,2,1,0:T(8,128)}, u32[]{:S(2)}, u32[]{:S(2)}) %all-to-all-start.1) | async-done | bytes 2621472 | tf_op jit(solution)/shard_map/all_to_all | solution.py:181
  117.6 2.1 %copy.35 = f32[32,5,16,256]{3,2,0,1:T(8,128)S(1)} copy(f32[32,5,16,256]{3,2,1,0:T(8,128)} %all-to-all-done.1) | data formatting | bytes 5242880 | tf_op jit(solution)/shard_map/all_to_all | solution.py:181
  119.7 1.4 slice_divide_fusion
  121.1 3.1 %copy.23 = f32[3,512,256]{1,2,0:T(8,128)} copy(f32[3,512,256]{2,1,0:T(8,128)} %bitcast.83) | data formatting | bytes 3145728 | tf_op jit(solution)/shard_map/reshape | solution.py:222
  124.2 17.0 %multiply_reduce_fusion = f32[8192,3]{0,1:T(4,128)S(1)} fusion(f32[8192,256]{0,1:T(8,128)} %fusion.11, f32[3,512,256]{1,2,0:T(8,128)} %copy.23, s32[8192]{0:T(1024)S(1)} %get-tuple-element.18), kind=kOutput, calls=%fused_computation.3 | convolution fusion | flops 19344105472 | bytes 10092544 | tf_op jit(solution)/shard_map/dot_general | solution.py:233
  141.9 18.3 %fusion = f32[512,3,256]{2,0,1:T(8,128)} fusion(f32[8192,3]{0,1:T(4,128)S(1)} %get-tuple-element.17, f32[8192,256]{0,1:T(8,128)} %fusion.11, s32[8192]{0:T(1024)S(1)} %get-tuple-element.18), kind=kOutput, calls=%fused_computation | convolution fusion | flops 19337838592 | bytes 10092544 | tf_op jit(solution)/shard_map/dot_general | solution.py:243
  160.2 1.8 slice_add_fusion
  163.4 1.9 fusion.44
  166.0 5.5 %collective-permute-start = (f32[7,2,16,256]{3,2,1,0:T(8,128)}, f32[7,2,16,256]{3,2,1,0:T(8,128)}, u32[]{:S(2)}, u32[]{:S(2)}) collective-permute-start(f32[7,2,16,256]{3,2,1,0:T(8,128)} %pad_maximum_fusion.2), channel_id=1, source_target_pairs={{0,32},{32,64},{64,96},{1,33},{33,65},{65,97},{2,34},{34,66},{66,9... | collective-permute-start | bytes 688136 | tf_op jit(solution)/shard_map/ppermute | solution.py:254
  171.5 0.7 pad_maximum_fusion.3
  172.2 1.9 collective-permute-start.1
  174.7 1.9 copy.27
  177.4 5.7 %collective-permute-start.3 = (f32[7,32,16,2]{1,2,3,0:T(8,128)S(1)}, f32[7,32,16,2]{1,2,3,0:T(8,128)S(1)}, u32[]{:S(2)}, u32[]{:S(2)}) collective-permute-start(f32[7,32,16,2]{1,2,3,0:T(8,128)S(1)} %pad_maximum_fusion.5), channel_id=1, source_target_pairs={{1,0},{2,1},{3,2},{4,3},{5,4},{6,5},{7,6},{8,7},{9,8},{10,9},{11,1... | collective-permute-start | bytes 86024 | tf_op jit(solution)/shard_map/ppermute | solution.py:269
  183.1 1.1 pad_maximum_fusion.1.s_ref
  184.9 2.0 copy.30.ah_ref
  186.9 2.0 copy.29.al_ref
  188.9 16.0 %shard_map.87 = f32[5,32,16,256]{3,2,1,0:T(8,128)} custom-call(f32[5,32,16,256]{3,2,1,0:T(8,128)} %copy-done, f32[2,32,16,256]{3,2,1,0:T(8,128)} %pad_maximum_fusion.1.s_ref, f32[7,2,16,256]{3,2,1,0:T(8,128)} %collective-permute-done.rl_ref, f32[7,2,16,256]{3,2,1,0:T(8,128)} %collective-permute-done.1.rh_ref, f32[7,32,16,2]{3,2,1,0:T(8,128)} %copy.29.al_ref, ...), custom_call_target="tpu_custom_call" | custom-call | tf_op jit(solution)/shard_map/pallas_call | solution.py:154
  (57 shorter events, 8.4 us)
Async XLA Ops:
  0.6 3.2 %copy-start.6 = (s32[4096,1]{0,1:T(1,128)S(1)}, s32[4096,1]{0,1:T(1,128)}, u32[]{:S(2)}) copy-start(s32[4096,1]{0,1:T(1,128)} %param.13) | copy-start | bytes 49156
  0.6 3.0 %copy-start.7 = (s32[4096]{0:T(1024)S(1)}, s32[4096]{0:T(1024)}, u32[]{:S(2)}) copy-start(s32[4096]{0:T(1024)} %param.12) | copy-start | bytes 49156
  0.7 3.1 %copy-start.8 = (f32[4096]{0:T(1024)S(1)}, f32[4096]{0:T(1024)}, u32[]{:S(2)}) copy-start(f32[4096]{0:T(1024)} %param.11) | copy-start | bytes 49156
  0.7 3.1 %copy-start.9 = (f32[4096]{0:T(1024)S(1)}, f32[4096]{0:T(1024)}, u32[]{:S(2)}) copy-start(f32[4096]{0:T(1024)} %param.10) | copy-start | bytes 49156
  0.7 3.1 %copy-start.5 = (f32[3,4096]{1,0:T(4,128)S(1)}, f32[3,4096]{1,0:T(4,128)}, u32[]{:S(2)}) copy-start(f32[3,4096]{1,0:T(4,128)} %param.9) | copy-start | bytes 147460
  3.9 16.2 %copy-start.4 = (f32[5,32,16,256]{3,2,1,0:T(8,128)S(1)}, f32[5,32,16,256]{3,2,1,0:T(8,128)}, u32[]{:S(2)}) copy-start(f32[5,32,16,256]{3,2,1,0:T(8,128)} %param.7) | copy-start | bytes 7864324
  8.6 21.7 %all-to-all-start.2 = ((f32[128,1,384]{2,1,0:T(1,128)}), f32[128,1,384]{2,1,0:T(1,128)S(1)}, u32[]{:S(2)}, u32[]{:S(2)}) async-start(f32[128,1,384]{2,1,0:T(1,128)} %reshape.194), calls=%async_computation.2 | async-start | bytes 393216 | tf_op jit(solution)/shard_map/all_to_all | solution.py:217
  30.3 4.2 %copy-start.10 = (s32[32]{0:T(128)S(1)}, s32[32]{0:T(128)}, u32[]{:S(2)}) copy-start(s32[32]{0:T(128)} %param.8) | copy-start | bytes 388
  30.3 38.6 %all-to-all-start = ((f32[32,5,16,256]{3,2,1,0:T(8,128)}), f32[32,5,16,256]{3,2,1,0:T(8,128)S(1)}, u32[]{:S(2)}, u32[]{:S(2)}) async-start(f32[32,5,16,256]{3,2,1,0:T(8,128)} %bitcast.76), calls=%async_computation | async-start | bytes 5242880 | tf_op jit(solution)/shard_map/all_to_all | solution.py:176
  68.9 1.5 copy-start.1
  77.4 40.2 %all-to-all-start.1 = ((f32[32,5,16,256]{3,2,1,0:T(8,128)}), f32[32,5,16,256]{3,2,1,0:T(8,128)}, u32[]{:S(2)}, u32[]{:S(2)}) async-start(f32[32,5,16,256]{3,2,1,0:T(8,128)} %bitcast.82), calls=%async_computation.1 | async-start | bytes 5242880 | tf_op jit(solution)/shard_map/all_to_all | solution.py:181
  162.2 0.8 copy-start.2
  163.4 1.9 copy-start
  165.3 17.8 %copy-start.3 = (f32[1,32,16,256]{3,2,1,0:T(8,128)S(1)}, f32[1,32,16,256]{3,2,1,0:T(8,128)}, u32[]{:S(2)}) copy-start(f32[1,32,16,256]{3,2,1,0:T(8,128)} %copy-done.2) | copy-start | bytes 1572868
  166.0 22.9 %collective-permute-start = (f32[7,2,16,256]{3,2,1,0:T(8,128)}, f32[7,2,16,256]{3,2,1,0:T(8,128)}, u32[]{:S(2)}, u32[]{:S(2)}) collective-permute-start(f32[7,2,16,256]{3,2,1,0:T(8,128)} %pad_maximum_fusion.2), channel_id=1, source_target_pairs={{0,32},{32,64},{64,96},{1,33},{33,65},{65,97},{2,34},{34,66},{66,9... | collective-permute-start | bytes 688136 | tf_op jit(solution)/shard_map/ppermute | solution.py:254
  172.2 16.7 %collective-permute-start.1 = (f32[7,2,16,256]{3,2,1,0:T(8,128)}, f32[7,2,16,256]{3,2,1,0:T(8,128)}, u32[]{:S(2)}, u32[]{:S(2)}) collective-permute-start(f32[7,2,16,256]{3,2,1,0:T(8,128)} %pad_maximum_fusion.3), channel_id=1, source_target_pairs={{32,0},{64,32},{96,64},{33,1},{65,33},{97,65},{34,2},{66,34},{98,6... | collective-permute-start | bytes 688136 | tf_op jit(solution)/shard_map/ppermute | solution.py:259
  177.3 9.6 %collective-permute-start.2 = (f32[7,32,16,2]{1,2,3,0:T(8,128)S(1)}, f32[7,32,16,2]{1,2,3,0:T(8,128)S(1)}, u32[]{:S(2)}, u32[]{:S(2)}) collective-permute-start(f32[7,32,16,2]{1,2,3,0:T(8,128)S(1)} %pad_maximum_fusion.4), channel_id=1, source_target_pairs={{0,1},{1,2},{2,3},{3,4},{4,5},{5,6},{6,7},{7,8},{8,9},{9,10},{10,1... | collective-permute-start | bytes 86024 | tf_op jit(solution)/shard_map/ppermute | solution.py:264
  177.4 7.5 %collective-permute-start.3 = (f32[7,32,16,2]{1,2,3,0:T(8,128)S(1)}, f32[7,32,16,2]{1,2,3,0:T(8,128)S(1)}, u32[]{:S(2)}, u32[]{:S(2)}) collective-permute-start(f32[7,32,16,2]{1,2,3,0:T(8,128)S(1)} %pad_maximum_fusion.5), channel_id=1, source_target_pairs={{1,0},{2,1},{3,2},{4,3},{5,4},{6,5},{7,6},{8,7},{9,8},{10,9},{11,1... | collective-permute-start | bytes 86024 | tf_op jit(solution)/shard_map/ppermute | solution.py:269

commit v3 on v2

--- a/solution.py
+++ b/solution.py
@@ -68,11 +68,32 @@
             whole = quotient_ref[i]
             part = remainder_ref[i]
 
+            tile = 128
+            tiles = sector // tile
+            offset = part // tile
+            within = part % tile
+            lane = lax.broadcasted_iota(jnp.int32, (rows, tile), 1)
+
             def body(s, carry):
                 current = ring_ref[(s - whole + sectors) % sectors, i]
                 preceding = ring_ref[(s - whole - 1 + 2 * sectors) % sectors, i]
-                window = jnp.concatenate([preceding, current], axis=-1)
-                out_ref[s, i] = pltpu.roll(window, part, 1)[:, sector:]
+                window = [preceding[:, t * tile : (t + 1) * tile] for t in range(tiles)] + [
+                    current[:, t * tile : (t + 1) * tile] for t in range(tiles)
+                ]
+
+                def pick(index):
+                    chosen = window[index]
+                    for back in range(1, tiles):
+                        if index - back >= 0:
+                            chosen = jnp.where(offset == back, window[index - back], chosen)
+                    return chosen
+
+                pieces = []
+                for t in range(tiles):
+                    upper = pltpu.roll(pick(tiles + t), within, 1)
+                    lower = pltpu.roll(pick(tiles + t - 1), within, 1)
+                    pieces.append(jnp.where(lane >= within, upper, lower))
+                out_ref[s, i] = jnp.concatenate(pieces, axis=-1)
                 return carry
 
             lax.fori_loop(0, sectors, body, 0)

time: 206 us -> 206 us (level)
  no operation moved by 1% of the time
where the time goes in v3:
time: 206 us; the launch traced here: 205 us
  waiting for transfers between devices  65.4 us (32%)
  matrix products  40.6 us (20%)
  starting transfers between devices  35.3 us (17%)
  local copies, waits for them, and re-layouts  22.8 us (11%)
  Pallas kernels  22.7 us (11%)
  other arithmetic  14.2 us (7%)
  between operations  3.61 us (2%)
    all_to_all x1, waiting for transfers between devices, local(): lax.all_to_all(rolled, 'sec', split_axis=0, concat_axis=0, tiled=True)  28.9 us
    all_to_all x1, waiting for transfers between devices, local(): lax.all_to_all(by_radius, 'sec', split_axis=0, concat_axis=0, tiled=True)  27.3 us
    dot_general x1, matrix products, local(): jnp.dot(row_hot.T, spread, precision=lax.Precision.HIGH, preferred_elemen...  18.3 us
    dot_general x1, matrix products, local(): jnp.dot(row_hot, velocity_rows, precision=lax.Precision.HIGH, preferred_e...  17 us
    pallas_call x1, Pallas kernels, transport(): pl.pallas_call(kernel, out_shape=jax.ShapeDtypeStruct(dragged.shape, drag...  16 us
    all_to_all x1, starting transfers between devices, local(): lax.all_to_all(outbox, ('rad', 'sec'), split_axis=0, concat_axis=0, tiled...  11.5 us
    all_to_all x1, waiting for transfers between devices, local(): lax.all_to_all(outbox, ('rad', 'sec'), split_axis=0, concat_axis=0, tiled...  8.44 us
    pallas_call x1, Pallas kernels, sector_roll(): pl.pallas_call(kernel, out_shape=jax.ShapeDtypeStruct(ring.shape, ring.dt...  6.68 us
  transfers between devices with their start and end apart: 7, of which 4 were waited for; matrix products, arithmetic and copies ran while one was open for 10% of the time, Pallas kernels for 0%

profile of v3, /device:TPU:1, one launch (start us, length us, event | category | flops | bytes accessed | tf_op | source)
XLA Modules:
  0.0 204.6 jit_solution(4350577266531037454)
XLA Ops:
  0.7 1.1 fusion.24
  2.0 1.6 fusion.18
  3.9 3.5 %fusion.12 = f32[128,6,64]{0,2,1:T(8,128)S(1)} fusion(f32[4096,6]{0,1:T(8,128)S(1)} %maximum_bitcast_fusion, pred[4096,64]{0,1:T(8,128)(4,1)S(1)} %iota_compare_fusion.7, s32[4096]{0:T(1024)S(1)} %bitcast.91), kind=kOutput, calls=%fused_computation.13 | convolution fusion | flops 2418016256 | bytes 573440 | tf_op jit(solution)/shard_map/dot_general | solution.py:235
  7.7 0.9 reshape.194
  8.6 11.5 %all-to-all-start.2 = ((f32[128,1,384]{2,1,0:T(1,128)}), f32[128,1,384]{2,1,0:T(1,128)S(1)}, u32[]{:S(2)}, u32[]{:S(2)}) async-start(f32[128,1,384]{2,1,0:T(1,128)} %reshape.194), calls=%async_computation.2 | async-start | bytes 393216 | tf_op jit(solution)/shard_map/all_to_all | solution.py:238
  20.1 1.7 copy.36
  21.8 8.4 %all-to-all-done.2 = f32[128,1,384]{2,1,0:T(1,128)S(1)} async-done(((f32[128,1,384]{2,1,0:T(1,128)}), f32[128,1,384]{2,1,0:T(1,128)S(1)}, u32[]{:S(2)}, u32[]{:S(2)}) %all-to-all-start.2) | async-done | bytes 196640 | tf_op jit(solution)/shard_map/all_to_all | solution.py:238
  30.3 4.2 %all-to-all-start = ((f32[32,5,16,256]{3,2,1,0:T(8,128)}), f32[32,5,16,256]{3,2,1,0:T(8,128)S(1)}, u32[]{:S(2)}, u32[]{:S(2)}) async-start(f32[32,5,16,256]{3,2,1,0:T(8,128)} %bitcast.76), calls=%async_computation | async-start | bytes 5242880 | tf_op jit(solution)/shard_map/all_to_all | solution.py:197
  38.2 1.1 reduce.14
  40.5 1.1 slice.65
  41.6 27.3 %all-to-all-done = f32[32,5,16,256]{3,2,1,0:T(8,128)S(1)} async-done(((f32[32,5,16,256]{3,2,1,0:T(8,128)}), f32[32,5,16,256]{3,2,1,0:T(8,128)S(1)}, u32[]{:S(2)}, u32[]{:S(2)}) %all-to-all-start) | async-done | bytes 2621472 | tf_op jit(solution)/shard_map/all_to_all | solution.py:197
  68.9 1.5 copy-done.1
  70.4 6.7 %shard_map.86 = f32[32,1,80,256]{3,2,1,0:T(8,128)} custom-call(s32[1]{0:T(128)S(6)} %select_n.48.quotient_ref, s32[1]{0:T(128)S(6)} %select_n.49.remainder_ref, f32[32,1,80,256]{3,2,1,0:T(8,128)} %bitcast.81), custom_call_target="tpu_custom_call" | custom-call | tf_op jit(solution)/shard_map/pallas_call | solution.py:101
  77.1 6.5 %all-to-all-start.1 = ((f32[32,5,16,256]{3,2,1,0:T(8,128)}), f32[32,5,16,256]{3,2,1,0:T(8,128)}, u32[]{:S(2)}, u32[]{:S(2)}) async-start(f32[32,5,16,256]{3,2,1,0:T(8,128)} %bitcast.82), calls=%async_computation.1 | async-start | bytes 5242880 | tf_op jit(solution)/shard_map/all_to_all | solution.py:202
  84.2 4.2 %fusion.11 = f32[8192,256]{0,1:T(8,128)} fusion(s32[8192]{0:T(1024)S(1)} %get-tuple-element.19), kind=kLoop, calls=%fused_computation.12 | loop fusion | flops 4194304 | bytes 8421376 | tf_op jit(solution)/shard_map/convert_element_type | solution.py:253
  88.4 28.9 %all-to-all-done.1 = f32[32,5,16,256]{3,2,1,0:T(8,128)} async-done(((f32[32,5,16,256]{3,2,1,0:T(8,128)}), f32[32,5,16,256]{3,2,1,0:T(8,128)}, u32[]{:S(2)}, u32[]{:S(2)}) %all-to-all-start.1) | async-done | bytes 2621472 | tf_op jit(solution)/shard_map/all_to_all | solution.py:202
  117.3 2.1 %copy.35 = f32[32,5,16,256]{3,2,0,1:T(8,128)S(1)} copy(f32[32,5,16,256]{3,2,1,0:T(8,128)} %all-to-all-done.1) | data formatting | bytes 5242880 | tf_op jit(solution)/shard_map/all_to_all | solution.py:202
  119.4 1.4 slice_divide_fusion
  120.8 3.1 %copy.23 = f32[3,512,256]{1,2,0:T(8,128)} copy(f32[3,512,256]{2,1,0:T(8,128)} %bitcast.83) | data formatting | bytes 3145728 | tf_op jit(solution)/shard_map/reshape | solution.py:243
  123.8 17.0 %multiply_reduce_fusion = f32[8192,3]{0,1:T(4,128)S(1)} fusion(f32[8192,256]{0,1:T(8,128)} %fusion.11, f32[3,512,256]{1,2,0:T(8,128)} %copy.23, s32[8192]{0:T(1024)S(1)} %get-tuple-element.18), kind=kOutput, calls=%fused_computation.3 | convolution fusion | flops 19344105472 | bytes 10092544 | tf_op jit(solution)/shard_map/dot_general | solution.py:254
  141.6 18.3 %fusion = f32[512,3,256]{2,0,1:T(8,128)} fusion(f32[8192,3]{0,1:T(4,128)S(1)} %get-tuple-element.17, f32[8192,256]{0,1:T(8,128)} %fusion.11, s32[8192]{0:T(1024)S(1)} %get-tuple-element.18), kind=kOutput, calls=%fused_computation | convolution fusion | flops 19337838592 | bytes 10092544 | tf_op jit(solution)/shard_map/dot_general | solution.py:264
  159.9 1.8 slice_add_fusion
  163.1 1.9 fusion.44
  165.7 5.4 %collective-permute-start = (f32[7,2,16,256]{3,2,1,0:T(8,128)}, f32[7,2,16,256]{3,2,1,0:T(8,128)}, u32[]{:S(2)}, u32[]{:S(2)}) collective-permute-start(f32[7,2,16,256]{3,2,1,0:T(8,128)} %pad_maximum_fusion.2), channel_id=1, source_target_pairs={{0,32},{32,64},{64,96},{1,33},{33,65},{65,97},{2,34},{34,66},{66,9... | collective-permute-start | bytes 688136 | tf_op jit(solution)/shard_map/ppermute | solution.py:275
  171.2 0.7 pad_maximum_fusion.3
  171.9 1.9 collective-permute-start.1
  174.4 1.9 copy.27
  177.0 5.7 %collective-permute-start.3 = (f32[7,32,16,2]{1,2,3,0:T(8,128)S(1)}, f32[7,32,16,2]{1,2,3,0:T(8,128)S(1)}, u32[]{:S(2)}, u32[]{:S(2)}) collective-permute-start(f32[7,32,16,2]{1,2,3,0:T(8,128)S(1)} %pad_maximum_fusion.5), channel_id=1, source_target_pairs={{1,0},{2,1},{3,2},{4,3},{5,4},{6,5},{7,6},{8,7},{9,8},{10,9},{11,1... | collective-permute-start | bytes 86024 | tf_op jit(solution)/shard_map/ppermute | solution.py:290
  182.8 1.1 pad_maximum_fusion.1.s_ref
  184.6 2.0 copy.30.ah_ref
  186.6 2.0 copy.29.al_ref
  188.6 16.0 %shard_map.87 = f32[5,32,16,256]{3,2,1,0:T(8,128)} custom-call(f32[5,32,16,256]{3,2,1,0:T(8,128)} %copy-done, f32[2,32,16,256]{3,2,1,0:T(8,128)} %pad_maximum_fusion.1.s_ref, f32[7,2,16,256]{3,2,1,0:T(8,128)} %collective-permute-done.rl_ref, f32[7,2,16,256]{3,2,1,0:T(8,128)} %collective-permute-done.1.rh_ref, f32[7,32,16,2]{3,2,1,0:T(8,128)} %copy.29.al_ref, ...), custom_call_target="tpu_custom_call" | custom-call | tf_op jit(solution)/shard_map/pallas_call | solution.py:175
  (57 shorter events, 8.4 us)
Async XLA Ops:
  0.6 3.2 %copy-start.6 = (s32[4096,1]{0,1:T(1,128)S(1)}, s32[4096,1]{0,1:T(1,128)}, u32[]{:S(2)}) copy-start(s32[4096,1]{0,1:T(1,128)} %param.13) | copy-start | bytes 49156
  0.6 3.0 %copy-start.7 = (s32[4096]{0:T(1024)S(1)}, s32[4096]{0:T(1024)}, u32[]{:S(2)}) copy-start(s32[4096]{0:T(1024)} %param.12) | copy-start | bytes 49156
  0.7 3.1 %copy-start.8 = (f32[4096]{0:T(1024)S(1)}, f32[4096]{0:T(1024)}, u32[]{:S(2)}) copy-start(f32[4096]{0:T(1024)} %param.11) | copy-start | bytes 49156
  0.7 3.1 %copy-start.9 = (f32[4096]{0:T(1024)S(1)}, f32[4096]{0:T(1024)}, u32[]{:S(2)}) copy-start(f32[4096]{0:T(1024)} %param.10) | copy-start | bytes 49156
  0.7 3.1 %copy-start.5 = (f32[3,4096]{1,0:T(4,128)S(1)}, f32[3,4096]{1,0:T(4,128)}, u32[]{:S(2)}) copy-start(f32[3,4096]{1,0:T(4,128)} %param.9) | copy-start | bytes 147460
  3.9 16.2 %copy-start.4 = (f32[5,32,16,256]{3,2,1,0:T(8,128)S(1)}, f32[5,32,16,256]{3,2,1,0:T(8,128)}, u32[]{:S(2)}) copy-start(f32[5,32,16,256]{3,2,1,0:T(8,128)} %param.7) | copy-start | bytes 7864324
  8.6 21.7 %all-to-all-start.2 = ((f32[128,1,384]{2,1,0:T(1,128)}), f32[128,1,384]{2,1,0:T(1,128)S(1)}, u32[]{:S(2)}, u32[]{:S(2)}) async-start(f32[128,1,384]{2,1,0:T(1,128)} %reshape.194), calls=%async_computation.2 | async-start | bytes 393216 | tf_op jit(solution)/shard_map/all_to_all | solution.py:238
  30.3 4.2 %copy-start.10 = (s32[32]{0:T(128)S(1)}, s32[32]{0:T(128)}, u32[]{:S(2)}) copy-start(s32[32]{0:T(128)} %param.8) | copy-start | bytes 388
  30.3 38.6 %all-to-all-start = ((f32[32,5,16,256]{3,2,1,0:T(8,128)}), f32[32,5,16,256]{3,2,1,0:T(8,128)S(1)}, u32[]{:S(2)}, u32[]{:S(2)}) async-start(f32[32,5,16,256]{3,2,1,0:T(8,128)} %bitcast.76), calls=%async_computation | async-start | bytes 5242880 | tf_op jit(solution)/shard_map/all_to_all | solution.py:197
  68.9 1.5 copy-start.1
  77.1 40.2 %all-to-all-start.1 = ((f32[32,5,16,256]{3,2,1,0:T(8,128)}), f32[32,5,16,256]{3,2,1,0:T(8,128)}, u32[]{:S(2)}, u32[]{:S(2)}) async-start(f32[32,5,16,256]{3,2,1,0:T(8,128)} %bitcast.82), calls=%async_computation.1 | async-start | bytes 5242880 | tf_op jit(solution)/shard_map/all_to_all | solution.py:202
  161.9 0.8 copy-start.2
  163.1 1.9 copy-start
  165.0 17.8 %copy-start.3 = (f32[1,32,16,256]{3,2,1,0:T(8,128)S(1)}, f32[1,32,16,256]{3,2,1,0:T(8,128)}, u32[]{:S(2)}) copy-start(f32[1,32,16,256]{3,2,1,0:T(8,128)} %copy-done.2) | copy-start | bytes 1572868
  165.7 22.9 %collective-permute-start = (f32[7,2,16,256]{3,2,1,0:T(8,128)}, f32[7,2,16,256]{3,2,1,0:T(8,128)}, u32[]{:S(2)}, u32[]{:S(2)}) collective-permute-start(f32[7,2,16,256]{3,2,1,0:T(8,128)} %pad_maximum_fusion.2), channel_id=1, source_target_pairs={{0,32},{32,64},{64,96},{1,33},{33,65},{65,97},{2,34},{34,66},{66,9... | collective-permute-start | bytes 688136 | tf_op jit(solution)/shard_map/ppermute | solution.py:275
  171.9 16.7 %collective-permute-start.1 = (f32[7,2,16,256]{3,2,1,0:T(8,128)}, f32[7,2,16,256]{3,2,1,0:T(8,128)}, u32[]{:S(2)}, u32[]{:S(2)}) collective-permute-start(f32[7,2,16,256]{3,2,1,0:T(8,128)} %pad_maximum_fusion.3), channel_id=1, source_target_pairs={{32,0},{64,32},{96,64},{33,1},{65,33},{97,65},{34,2},{66,34},{98,6... | collective-permute-start | bytes 688136 | tf_op jit(solution)/shard_map/ppermute | solution.py:280
  176.9 9.6 %collective-permute-start.2 = (f32[7,32,16,2]{1,2,3,0:T(8,128)S(1)}, f32[7,32,16,2]{1,2,3,0:T(8,128)S(1)}, u32[]{:S(2)}, u32[]{:S(2)}) collective-permute-start(f32[7,32,16,2]{1,2,3,0:T(8,128)S(1)} %pad_maximum_fusion.4), channel_id=1, source_target_pairs={{0,1},{1,2},{2,3},{3,4},{4,5},{5,6},{6,7},{7,8},{8,9},{9,10},{10,1... | collective-permute-start | bytes 86024 | tf_op jit(solution)/shard_map/ppermute | solution.py:285
  177.0 7.5 %collective-permute-start.3 = (f32[7,32,16,2]{1,2,3,0:T(8,128)S(1)}, f32[7,32,16,2]{1,2,3,0:T(8,128)S(1)}, u32[]{:S(2)}, u32[]{:S(2)}) collective-permute-start(f32[7,32,16,2]{1,2,3,0:T(8,128)S(1)} %pad_maximum_fusion.5), channel_id=1, source_target_pairs={{1,0},{2,1},{3,2},{4,3},{5,4},{6,5},{7,6},{8,7},{9,8},{10,9},{11,1... | collective-permute-start | bytes 86024 | tf_op jit(solution)/shard_map/ppermute | solution.py:290

commit v4 on v3

--- a/solution.py
+++ b/solution.py
@@ -235,6 +235,7 @@
     outbox = jnp.dot(
         hits.astype(jnp.float32).T, spread_records, precision=exact, preferred_element_type=jnp.float32
     ).reshape(devices, 6, capacity)
+    outbox, _ = lax.optimization_barrier((outbox, ring))
     inbox = lax.all_to_all(outbox, ("rad", "sec"), split_axis=0, concat_axis=0, tiled=True)
     received = inbox.transpose(1, 0, 2).reshape(6, devices * capacity)
     row_count = radius_count * layers

time: 206 us -> 199 us (0.966)
  waiting for transfers between devices: 65.4 us -> 56.1 us
  starting transfers between devices: 35.3 us -> 40.6 us
    all_to_all x1, waiting for transfers between devices: 8.44 us -> 0.3 us  [local(): lax.all_to_all(outbox, ('rad', 'sec'), split_axis=0, concat_axis=0, tiled...]
    all_to_all x1, starting transfers between devices: 4.19 us -> 9.93 us  [local(): lax.all_to_all(by_radius, 'sec', split_axis=0, concat_axis=0, tiled=True)]
    all_to_all x1, starting transfers between devices: 11.5 us -> 8.35 us  [local(): lax.all_to_all(outbox, ('rad', 'sec'), split_axis=0, concat_axis=0, tiled...]
    all_to_all x1, waiting for transfers between devices: 28.9 us -> 25.9 us  [local(): lax.all_to_all(rolled, 'sec', split_axis=0, concat_axis=0, tiled=True)]
    unnamed x25 -> x23, local copies, waits for them, and re-layouts: 4.89 us -> 5.55 us
  transfers between devices with their start and end apart: 7 -> 7, of which waited for: 4 -> 4; matrix products, arithmetic and copies ran while one was open for 10% -> 11% of each run, Pallas kernels for 0% -> 3%
where the time goes in v4:
time: 199 us; the launch traced here: 198 us
  waiting for transfers between devices  56.1 us (28%)
  starting transfers between devices  40.6 us (20%)
  matrix products  39.8 us (20%)
  Pallas kernels  22.7 us (11%)
  local copies, waits for them, and re-layouts  21.9 us (11%)
  other arithmetic  13.4 us (7%)
  between operations  3.6 us (2%)
    all_to_all x1, waiting for transfers between devices, local(): lax.all_to_all(by_radius, 'sec', split_axis=0, concat_axis=0, tiled=True)  29.1 us
    all_to_all x1, waiting for transfers between devices, local(): lax.all_to_all(rolled, 'sec', split_axis=0, concat_axis=0, tiled=True)  25.9 us
    dot_general x1, matrix products, local(): jnp.dot(row_hot.T, spread, precision=lax.Precision.HIGH, preferred_elemen...  18.3 us
    dot_general x1, matrix products, local(): jnp.dot(row_hot, velocity_rows, precision=lax.Precision.HIGH, preferred_e...  17 us
    pallas_call x1, Pallas kernels, transport(): pl.pallas_call(kernel, out_shape=jax.ShapeDtypeStruct(dragged.shape, drag...  16 us
    all_to_all x1, starting transfers between devices, local(): lax.all_to_all(by_radius, 'sec', split_axis=0, concat_axis=0, tiled=True)  9.93 us
    all_to_all x1, starting transfers between devices, local(): lax.all_to_all(rolled, 'sec', split_axis=0, concat_axis=0, tiled=True)  8.38 us
    all_to_all x1, starting transfers between devices, local(): lax.all_to_all(outbox, ('rad', 'sec'), split_axis=0, concat_axis=0, tiled...  8.35 us
  transfers between devices with their start and end apart: 7, of which 4 were waited for; matrix products, arithmetic and copies ran while one was open for 11% of the time, Pallas kernels for 3%

profile of v4, /device:TPU:1, one launch (start us, length us, event | category | flops | bytes accessed | tf_op | source)
XLA Modules:
  0.0 198.0 jit_solution(6820944399729226759)
XLA Ops:
  0.6 3.5 %copy.36 = f32[5,32,16,256]{3,2,0,1:T(8,128)} copy(f32[5,32,16,256]{3,2,1,0:T(8,128)} %param.7) | data formatting | bytes 5242880 | tf_op args[0]
  4.1 9.9 %all-to-all-start = ((f32[32,5,16,256]{3,2,1,0:T(8,128)}), f32[32,5,16,256]{3,2,1,0:T(8,128)S(1)}, u32[]{:S(2)}, u32[]{:S(2)}) async-start(f32[32,5,16,256]{3,2,1,0:T(8,128)} %bitcast.83), calls=%async_computation | async-start | bytes 5242880 | tf_op jit(solution)/shard_map/all_to_all | solution.py:197
  14.6 0.8 fusion.18
  15.7 3.5 %fusion.12 = f32[128,6,64]{0,2,1:T(8,128)S(1)} fusion(f32[4096,6]{0,1:T(8,128)S(1)} %maximum_bitcast_fusion, pred[4096,64]{0,1:T(8,128)(4,1)S(1)} %iota_compare_fusion.7, s32[4096]{0:T(1024)S(1)} %bitcast.92), kind=kOutput, calls=%fused_computation.13 | convolution fusion | flops 2418016256 | bytes 573440 | tf_op jit(solution)/shard_map/dot_general | solution.py:235
  19.3 29.1 %all-to-all-done = f32[32,5,16,256]{3,2,1,0:T(8,128)S(1)} async-done(((f32[32,5,16,256]{3,2,1,0:T(8,128)}), f32[32,5,16,256]{3,2,1,0:T(8,128)S(1)}, u32[]{:S(2)}, u32[]{:S(2)}) %all-to-all-start) | async-done | bytes 2621472 | tf_op jit(solution)/shard_map/all_to_all | solution.py:197
  48.7 1.3 reshape.194
  49.9 8.3 %all-to-all-start.2 = ((f32[128,1,384]{2,1,0:T(1,128)}), f32[128,1,384]{2,1,0:T(1,128)S(1)}, u32[]{:S(2)}, u32[]{:S(2)}) async-start(f32[128,1,384]{2,1,0:T(1,128)} %reshape.194), calls=%async_computation.2 | async-start | bytes 393216 | tf_op jit(solution)/shard_map/all_to_all | solution.py:239
  61.5 6.7 %shard_map.86 = f32[32,1,80,256]{3,2,1,0:T(8,128)} custom-call(s32[1]{0:T(128)S(6)} %select_n.48.quotient_ref, s32[1]{0:T(128)S(6)} %select_n.49.remainder_ref, f32[32,1,80,256]{3,2,1,0:T(8,128)} %bitcast.81), custom_call_target="tpu_custom_call" | custom-call | tf_op jit(solution)/shard_map/pallas_call | solution.py:101
  68.5 8.4 %all-to-all-start.1 = ((f32[32,5,16,256]{3,2,1,0:T(8,128)}), f32[32,5,16,256]{3,2,1,0:T(8,128)}, u32[]{:S(2)}, u32[]{:S(2)}) async-start(f32[32,5,16,256]{3,2,1,0:T(8,128)} %bitcast.82), calls=%async_computation.1 | async-start | bytes 5242880 | tf_op jit(solution)/shard_map/all_to_all | solution.py:202
  77.4 1.1 reduce.14
  79.8 4.2 %fusion.11 = f32[8192,256]{0,1:T(8,128)} fusion(s32[8192]{0:T(1024)S(1)} %get-tuple-element.21), kind=kLoop, calls=%fused_computation.12 | loop fusion | flops 4194304 | bytes 8421376 | tf_op jit(solution)/shard_map/convert_element_type | solution.py:254
  84.0 25.9 %all-to-all-done.1 = f32[32,5,16,256]{3,2,1,0:T(8,128)} async-done(((f32[32,5,16,256]{3,2,1,0:T(8,128)}), f32[32,5,16,256]{3,2,1,0:T(8,128)}, u32[]{:S(2)}, u32[]{:S(2)}) %all-to-all-start.1) | async-done | bytes 2621472 | tf_op jit(solution)/shard_map/all_to_all | solution.py:202
  109.9 2.1 %copy.35 = f32[32,5,16,256]{3,2,0,1:T(8,128)S(1)} copy(f32[32,5,16,256]{3,2,1,0:T(8,128)} %all-to-all-done.1) | data formatting | bytes 5242880 | tf_op jit(solution)/shard_map/all_to_all | solution.py:202
  112.0 1.4 slice_divide_fusion
  113.4 3.1 %copy.23 = f32[3,512,256]{1,2,0:T(8,128)} copy(f32[3,512,256]{2,1,0:T(8,128)} %bitcast.84) | data formatting | bytes 3145728 | tf_op jit(solution)/shard_map/reshape | solution.py:244
  116.5 17.0 %multiply_reduce_fusion = f32[8192,3]{0,1:T(4,128)S(1)} fusion(f32[8192,256]{0,1:T(8,128)} %fusion.11, f32[3,512,256]{1,2,0:T(8,128)} %copy.23, s32[8192]{0:T(1024)S(1)} %get-tuple-element.20), kind=kOutput, calls=%fused_computation.3 | convolution fusion | flops 19344105472 | bytes 10092544 | tf_op jit(solution)/shard_map/dot_general | solution.py:255
  133.5 0.7 fusion.34
  134.2 18.3 %fusion = f32[512,3,256]{2,0,1:T(8,128)} fusion(f32[8192,3]{0,1:T(4,128)S(1)} %get-tuple-element.19, f32[8192,256]{0,1:T(8,128)} %fusion.11, s32[8192]{0:T(1024)S(1)} %get-tuple-element.20), kind=kOutput, calls=%fused_computation | convolution fusion | flops 19337838592 | bytes 10092544 | tf_op jit(solution)/shard_map/dot_general | solution.py:265
  152.5 1.8 slice_add_fusion
  155.8 1.9 fusion.44
  157.7 0.7 pad_maximum_fusion.2
  158.4 6.2 %collective-permute-start = (f32[7,2,16,256]{3,2,1,0:T(8,128)}, f32[7,2,16,256]{3,2,1,0:T(8,128)}, u32[]{:S(2)}, u32[]{:S(2)}) collective-permute-start(f32[7,2,16,256]{3,2,1,0:T(8,128)} %pad_maximum_fusion.2), channel_id=1, source_target_pairs={{0,32},{32,64},{64,96},{1,33},{33,65},{65,97},{2,34},{34,66},{66,9... | collective-permute-start | bytes 688136 | tf_op jit(solution)/shard_map/ppermute | solution.py:276
  164.6 0.7 pad_maximum_fusion.3
  165.3 1.9 collective-permute-start.1
  167.8 1.9 copy.27
  169.7 0.6 copy.25
  170.5 5.7 %collective-permute-start.3 = (f32[7,32,16,2]{1,2,3,0:T(8,128)S(1)}, f32[7,32,16,2]{1,2,3,0:T(8,128)S(1)}, u32[]{:S(2)}, u32[]{:S(2)}) collective-permute-start(f32[7,32,16,2]{1,2,3,0:T(8,128)S(1)} %pad_maximum_fusion.5), channel_id=1, source_target_pairs={{1,0},{2,1},{3,2},{4,3},{5,4},{6,5},{7,6},{8,7},{9,8},{10,9},{11,1... | collective-permute-start | bytes 86024 | tf_op jit(solution)/shard_map/ppermute | solution.py:291
  176.2 1.1 pad_maximum_fusion.1.s_ref
  177.3 0.7 collective-permute-done.3
  178.0 2.0 %copy.30.ah_ref = f32[7,32,16,2]{3,2,1,0:T(8,128)} copy(f32[7,32,16,2]{1,2,3,0:T(8,128)S(1)} %collective-permute-done.3) | data formatting | bytes 57344 | tf_op jit(solution)/shard_map/ppermute | solution.py:291
  180.0 2.0 copy.29.al_ref
  182.0 16.0 %shard_map.87 = f32[5,32,16,256]{3,2,1,0:T(8,128)} custom-call(f32[5,32,16,256]{3,2,1,0:T(8,128)} %copy-done, f32[2,32,16,256]{3,2,1,0:T(8,128)} %pad_maximum_fusion.1.s_ref, f32[7,2,16,256]{3,2,1,0:T(8,128)} %collective-permute-done.rl_ref, f32[7,2,16,256]{3,2,1,0:T(8,128)} %collective-permute-done.1.rh_ref, f32[7,32,16,2]{3,2,1,0:T(8,128)} %copy.29.al_ref, ...), custom_call_target="tpu_custom_call" | custom-call | tf_op jit(solution)/shard_map/pallas_call | solution.py:175
  (55 shorter events, 5.8 us)
Async XLA Ops:
  4.1 9.9 %copy-start.6 = (s32[4096]{0:T(1024)S(1)}, s32[4096]{0:T(1024)}, u32[]{:S(2)}) copy-start(s32[4096]{0:T(1024)} %param.12) | copy-start | bytes 49156
  4.1 10.0 %copy-start.5 = (s32[4096,1]{0,1:T(1,128)S(1)}, s32[4096,1]{0,1:T(1,128)}, u32[]{:S(2)}) copy-start(s32[4096,1]{0,1:T(1,128)} %param.13) | copy-start | bytes 49156
  4.1 44.3 %all-to-all-start = ((f32[32,5,16,256]{3,2,1,0:T(8,128)}), f32[32,5,16,256]{3,2,1,0:T(8,128)S(1)}, u32[]{:S(2)}, u32[]{:S(2)}) async-start(f32[32,5,16,256]{3,2,1,0:T(8,128)} %bitcast.83), calls=%async_computation | async-start | bytes 5242880 | tf_op jit(solution)/shard_map/all_to_all | solution.py:197
  14.1 1.4 copy-start.4
  14.1 1.4 copy-start.7
  14.1 1.4 copy-start.8
  15.7 42.6 %copy-start.9 = (s32[32]{0:T(128)S(1)}, s32[32]{0:T(128)}, u32[]{:S(2)}) copy-start(s32[32]{0:T(128)} %param.8) | copy-start | bytes 388
  48.4 13.1 %copy-start.1 = (f32[32,5,16,256]{3,2,1,0:T(8,128)}, f32[32,5,16,256]{3,2,1,0:T(8,128)S(1)}, u32[]{:S(2)}) copy-start(f32[32,5,16,256]{3,2,1,0:T(8,128)S(1)} %all-to-all-done) | copy-start | bytes 7864324
  49.9 18.5 %all-to-all-start.2 = ((f32[128,1,384]{2,1,0:T(1,128)}), f32[128,1,384]{2,1,0:T(1,128)S(1)}, u32[]{:S(2)}, u32[]{:S(2)}) async-start(f32[128,1,384]{2,1,0:T(1,128)} %reshape.194), calls=%async_computation.2 | async-start | bytes 393216 | tf_op jit(solution)/shard_map/all_to_all | solution.py:239
  68.5 41.4 %all-to-all-start.1 = ((f32[32,5,16,256]{3,2,1,0:T(8,128)}), f32[32,5,16,256]{3,2,1,0:T(8,128)}, u32[]{:S(2)}, u32[]{:S(2)}) async-start(f32[32,5,16,256]{3,2,1,0:T(8,128)} %bitcast.82), calls=%async_computation.1 | async-start | bytes 5242880 | tf_op jit(solution)/shard_map/all_to_all | solution.py:202
  154.5 0.8 copy-start.2
  155.7 2.0 copy-start
  157.7 18.5 %copy-start.3 = (f32[1,32,16,256]{3,2,1,0:T(8,128)S(1)}, f32[1,32,16,256]{3,2,1,0:T(8,128)}, u32[]{:S(2)}) copy-start(f32[1,32,16,256]{3,2,1,0:T(8,128)} %copy-done.2) | copy-start | bytes 1572868
  158.4 23.6 %collective-permute-start = (f32[7,2,16,256]{3,2,1,0:T(8,128)}, f32[7,2,16,256]{3,2,1,0:T(8,128)}, u32[]{:S(2)}, u32[]{:S(2)}) collective-permute-start(f32[7,2,16,256]{3,2,1,0:T(8,128)} %pad_maximum_fusion.2), channel_id=1, source_target_pairs={{0,32},{32,64},{64,96},{1,33},{33,65},{65,97},{2,34},{34,66},{66,9... | collective-permute-start | bytes 688136 | tf_op jit(solution)/shard_map/ppermute | solution.py:276
  165.3 16.7 %collective-permute-start.1 = (f32[7,2,16,256]{3,2,1,0:T(8,128)}, f32[7,2,16,256]{3,2,1,0:T(8,128)}, u32[]{:S(2)}, u32[]{:S(2)}) collective-permute-start(f32[7,2,16,256]{3,2,1,0:T(8,128)} %pad_maximum_fusion.3), channel_id=1, source_target_pairs={{32,0},{64,32},{96,64},{33,1},{65,33},{97,65},{34,2},{66,34},{98,6... | collective-permute-start | bytes 688136 | tf_op jit(solution)/shard_map/ppermute | solution.py:281
  170.4 9.6 %collective-permute-start.2 = (f32[7,32,16,2]{1,2,3,0:T(8,128)S(1)}, f32[7,32,16,2]{1,2,3,0:T(8,128)S(1)}, u32[]{:S(2)}, u32[]{:S(2)}) collective-permute-start(f32[7,32,16,2]{1,2,3,0:T(8,128)S(1)} %pad_maximum_fusion.4), channel_id=1, source_target_pairs={{0,1},{1,2},{2,3},{3,4},{4,5},{5,6},{6,7},{7,8},{8,9},{9,10},{10,1... | collective-permute-start | bytes 86024 | tf_op jit(solution)/shard_map/ppermute | solution.py:286
  170.5 7.5 %collective-permute-start.3 = (f32[7,32,16,2]{1,2,3,0:T(8,128)S(1)}, f32[7,32,16,2]{1,2,3,0:T(8,128)S(1)}, u32[]{:S(2)}, u32[]{:S(2)}) collective-permute-start(f32[7,32,16,2]{1,2,3,0:T(8,128)S(1)} %pad_maximum_fusion.5), channel_id=1, source_target_pairs={{1,0},{2,1},{3,2},{4,3},{5,4},{6,5},{7,6},{8,7},{9,8},{10,9},{11,1... | collective-permute-start | bytes 86024 | tf_op jit(solution)/shard_map/ppermute | solution.py:291

commit v5 on v4

--- a/solution.py
+++ b/solution.py
@@ -129,23 +129,30 @@
     def kernel(d_ref, s_ref, rl_ref, rh_ref, al_ref, ah_ref, out_ref):
         lane = lax.broadcasted_iota(jnp.int32, (layers, cells), 1)
 
+        def edge_of(ref, f, component, *index):
+            if f < fields:
+                return ref[(f,) + index]
+            density = ref[(0,) + index]
+            safe = jnp.where(density == 0, 1.0, density)
+            return jnp.where(density == 0, 0.0, ref[(component,) + index] / safe)
+
         def radial_at(f, r, offset):
             k = r + offset
             inner = d_ref[f, jnp.clip(k, 0, radii - 1)] if f < fields else s_ref[0, jnp.clip(k, 0, radii - 1)]
-            low = rl_ref[f, jnp.clip(k + 2, 0, 1)]
-            high = rh_ref[f, jnp.clip(k - radii, 0, 1)]
+            low = edge_of(rl_ref, f, 1, jnp.clip(k + 2, 0, 1))
+            high = edge_of(rh_ref, f, 1, jnp.clip(k - radii, 0, 1))
             return jnp.where(k < 0, low, jnp.where(k >= radii, high, inner))
 
         def ring_at(centre, f, r, offset):
             if offset < 0:
                 moved = pltpu.roll(centre, -offset, 1)
                 for j in range(-offset):
-                    edge = al_ref[f, r, :, 2 + offset + j : 3 + offset + j]
+                    edge = edge_of(al_ref, f, 2, r, slice(None), slice(2 + offset + j, 3 + offset + j))
                     moved = jnp.where(lane == j, edge, moved)
             else:
                 moved = pltpu.roll(centre, cells - offset, 1)
                 for j in range(offset):
-                    edge = ah_ref[f, r, :, j : j + 1]
+                    edge = edge_of(ah_ref, f, 2, r, slice(None), slice(j, j + 1))
                     moved = jnp.where(lane == cells - offset + j, edge, moved)
             return moved
 
@@ -274,22 +281,22 @@
     speeds = jnp.stack([radial_speed, azimuthal_speed], axis=0)
     rads = lax.axis_size("rad")
     radial_low = lax.ppermute(
-        jnp.concatenate([dragged[:, -2:], speeds[:, -2:]], axis=0),
+        dragged[:, -2:],
         "rad",
         [(i, i + 1) for i in range(rads - 1)],
     )
     radial_high = lax.ppermute(
-        jnp.concatenate([dragged[:, :2], speeds[:, :2]], axis=0),
+        dragged[:, :2],
         "rad",
         [(i + 1, i) for i in range(rads - 1)],
     )
     ring_low = lax.ppermute(
-        jnp.concatenate([dragged[..., -2:], speeds[..., -2:]], axis=0),
+        dragged[..., -2:],
         "sec",
         [(i, (i + 1) % sectors) for i in range(sectors)],
     )
     ring_high = lax.ppermute(
-        jnp.concatenate([dragged[..., :2], speeds[..., :2]], axis=0),
+        dragged[..., :2],
         "sec",
         [((i + 1) % sectors, i) for i in range(sectors)],
     )

time: 199 us -> 193 us (0.970)
  local copies, waits for them, and re-layouts: 21.9 us -> 17.2 us
    slice x2, local copies, waits for them, and re-layouts: 3.78 us -> 1.07 us  [local(): dragged[..., :2]]
    unnamed x23 -> x19, local copies, waits for them, and re-layouts: 5.55 us -> 4.92 us
  transfers between devices with their start and end apart: 7 -> 7, of which waited for: 4 -> 3; matrix products, arithmetic and copies ran while one was open for 11% -> 10% of each run, Pallas kernels for 3% -> 3%
where the time goes in v5:
time: 193 us; the launch traced here: 192 us
  waiting for transfers between devices  55.4 us (29%)
  starting transfers between devices  40.5 us (21%)
  matrix products  39.8 us (21%)
  Pallas kernels  22.3 us (12%)
  local copies, waits for them, and re-layouts  17.2 us (9%)
  other arithmetic  13.6 us (7%)
  between operations  3.57 us (2%)
    all_to_all x1, waiting for transfers between devices, local(): lax.all_to_all(by_radius, 'sec', split_axis=0, concat_axis=0, tiled=True)  29.1 us
    all_to_all x1, waiting for transfers between devices, local(): lax.all_to_all(rolled, 'sec', split_axis=0, concat_axis=0, tiled=True)  26 us
    dot_general x1, matrix products, local(): jnp.dot(row_hot.T, spread, precision=lax.Precision.HIGH, preferred_elemen...  18.3 us
    dot_general x1, matrix products, local(): jnp.dot(row_hot, velocity_rows, precision=lax.Precision.HIGH, preferred_e...  17 us
    pallas_call x1, Pallas kernels, transport(): pl.pallas_call(kernel, out_shape=jax.ShapeDtypeStruct(dragged.shape, drag...  15.6 us
    all_to_all x1, starting transfers between devices, local(): lax.all_to_all(by_radius, 'sec', split_axis=0, concat_axis=0, tiled=True)  9.93 us
    all_to_all x1, starting transfers between devices, local(): lax.all_to_all(rolled, 'sec', split_axis=0, concat_axis=0, tiled=True)  8.36 us
    all_to_all x1, starting transfers between devices, local(): lax.all_to_all(outbox, ('rad', 'sec'), split_axis=0, concat_axis=0, tiled...  8.35 us
  transfers between devices with their start and end apart: 7, of which 3 were waited for; matrix products, arithmetic and copies ran while one was open for 10% of the time, Pallas kernels for 3%

profile of v5, /device:TPU:1, one launch (start us, length us, event | category | flops | bytes accessed | tf_op | source)
XLA Modules:
  0.0 192.3 jit_solution(7550277751304772166)
XLA Ops:
  0.6 3.5 %copy.34 = f32[5,32,16,256]{3,2,0,1:T(8,128)} copy(f32[5,32,16,256]{3,2,1,0:T(8,128)} %param.7) | data formatting | bytes 5242880 | tf_op args[0]
  4.1 9.9 %all-to-all-start = ((f32[32,5,16,256]{3,2,1,0:T(8,128)}), f32[32,5,16,256]{3,2,1,0:T(8,128)S(1)}, u32[]{:S(2)}, u32[]{:S(2)}) async-start(f32[32,5,16,256]{3,2,1,0:T(8,128)} %bitcast.83), calls=%async_computation | async-start | bytes 5242880 | tf_op jit(solution)/shard_map/all_to_all | solution.py:204
  14.6 0.8 fusion.18
  15.7 3.5 %fusion.12 = f32[128,6,64]{0,2,1:T(8,128)S(1)} fusion(f32[4096,6]{0,1:T(8,128)S(1)} %maximum_bitcast_fusion, pred[4096,64]{0,1:T(8,128)(4,1)S(1)} %iota_compare_fusion.7, s32[4096]{0:T(1024)S(1)} %bitcast.92), kind=kOutput, calls=%fused_computation.13 | convolution fusion | flops 2418016256 | bytes 573440 | tf_op jit(solution)/shard_map/dot_general | solution.py:242
  19.3 29.1 %all-to-all-done = f32[32,5,16,256]{3,2,1,0:T(8,128)S(1)} async-done(((f32[32,5,16,256]{3,2,1,0:T(8,128)}), f32[32,5,16,256]{3,2,1,0:T(8,128)S(1)}, u32[]{:S(2)}, u32[]{:S(2)}) %all-to-all-start) | async-done | bytes 2621472 | tf_op jit(solution)/shard_map/all_to_all | solution.py:204
  48.7 1.3 reshape.194
  49.9 8.3 %all-to-all-start.2 = ((f32[128,1,384]{2,1,0:T(1,128)}), f32[128,1,384]{2,1,0:T(1,128)S(1)}, u32[]{:S(2)}, u32[]{:S(2)}) async-start(f32[128,1,384]{2,1,0:T(1,128)} %reshape.194), calls=%async_computation.2 | async-start | bytes 393216 | tf_op jit(solution)/shard_map/all_to_all | solution.py:246
  58.3 0.6 dynamic_slice.3
  61.5 6.6 %shard_map.86 = f32[32,1,80,256]{3,2,1,0:T(8,128)} custom-call(s32[1]{0:T(128)S(6)} %select_n.48.quotient_ref, s32[1]{0:T(128)S(6)} %select_n.49.remainder_ref, f32[32,1,80,256]{3,2,1,0:T(8,128)} %bitcast.81), custom_call_target="tpu_custom_call" | custom-call | tf_op jit(solution)/shard_map/pallas_call | solution.py:101
  68.5 8.4 %all-to-all-start.1 = ((f32[32,5,16,256]{3,2,1,0:T(8,128)}), f32[32,5,16,256]{3,2,1,0:T(8,128)}, u32[]{:S(2)}, u32[]{:S(2)}) async-start(f32[32,5,16,256]{3,2,1,0:T(8,128)} %bitcast.82), calls=%async_computation.1 | async-start | bytes 5242880 | tf_op jit(solution)/shard_map/all_to_all | solution.py:209
  76.8 0.5 broadcast.137
  77.4 1.1 reduce.14
  79.7 4.2 %fusion.11 = f32[8192,256]{0,1:T(8,128)} fusion(s32[8192]{0:T(1024)S(1)} %get-tuple-element.17), kind=kLoop, calls=%fused_computation.12 | loop fusion | flops 4194304 | bytes 8421376 | tf_op jit(solution)/shard_map/convert_element_type | solution.py:261
  83.9 26.0 %all-to-all-done.1 = f32[32,5,16,256]{3,2,1,0:T(8,128)} async-done(((f32[32,5,16,256]{3,2,1,0:T(8,128)}), f32[32,5,16,256]{3,2,1,0:T(8,128)}, u32[]{:S(2)}, u32[]{:S(2)}) %all-to-all-start.1) | async-done | bytes 2621472 | tf_op jit(solution)/shard_map/all_to_all | solution.py:209
  109.9 2.1 %copy.33 = f32[32,5,16,256]{3,2,0,1:T(8,128)S(1)} copy(f32[32,5,16,256]{3,2,1,0:T(8,128)} %all-to-all-done.1) | data formatting | bytes 5242880 | tf_op jit(solution)/shard_map/all_to_all | solution.py:209
  112.0 1.4 slice_divide_fusion
  113.4 3.1 %copy.23 = f32[3,512,256]{1,2,0:T(8,128)} copy(f32[3,512,256]{2,1,0:T(8,128)} %bitcast.84) | data formatting | bytes 3145728 | tf_op jit(solution)/shard_map/reshape | solution.py:251
  116.5 17.0 %multiply_reduce_fusion = f32[8192,3]{0,1:T(4,128)S(1)} fusion(f32[8192,256]{0,1:T(8,128)} %fusion.11, f32[3,512,256]{1,2,0:T(8,128)} %copy.23, s32[8192]{0:T(1024)S(1)} %get-tuple-element.16), kind=kOutput, calls=%fused_computation.3 | convolution fusion | flops 19344105472 | bytes 10092544 | tf_op jit(solution)/shard_map/dot_general | solution.py:262
  133.5 0.7 fusion.32
  134.2 18.3 %fusion = f32[512,3,256]{2,0,1:T(8,128)} fusion(f32[8192,3]{0,1:T(4,128)S(1)} %get-tuple-element.15, f32[8192,256]{0,1:T(8,128)} %fusion.11, s32[8192]{0:T(1024)S(1)} %get-tuple-element.16), kind=kOutput, calls=%fused_computation | convolution fusion | flops 19337838592 | bytes 10092544 | tf_op jit(solution)/shard_map/dot_general | solution.py:272
  152.6 1.8 slice_add_fusion
  154.3 1.0 slice_divide_fusion.2
  155.8 3.9 %collective-permute-start.1 = (f32[5,2,16,256]{3,2,1,0:T(8,128)S(1)}, f32[5,2,16,256]{3,2,1,0:T(8,128)}, u32[]{:S(2)}, u32[]{:S(2)}) collective-permute-start(f32[5,2,16,256]{3,2,1,0:T(8,128)S(1)} %get-tuple-element.10), channel_id=1, source_target_pairs={{32,0},{64,32},{96,64},{33,1},{65,33},{97,65},{34,2},{66,34},{98,6... | collective-permute-start | bytes 491528 | tf_op jit(solution)/shard_map/ppermute | solution.py:288
  159.7 4.2 %collective-permute-start = (f32[5,2,16,256]{3,2,1,0:T(8,128)S(1)}, f32[5,2,16,256]{3,2,1,0:T(8,128)}, u32[]{:S(2)}, u32[]{:S(2)}) collective-permute-start(f32[5,2,16,256]{3,2,1,0:T(8,128)S(1)} %get-tuple-element.11), channel_id=1, source_target_pairs={{0,32},{32,64},{64,96},{1,33},{33,65},{65,97},{2,34},{34,66},{66,9... | collective-permute-start | bytes 491528 | tf_op jit(solution)/shard_map/ppermute | solution.py:283
  163.9 0.4 fusion.40
  164.4 0.6 copy.26
  165.0 0.6 copy.25
  165.7 5.7 %collective-permute-start.3 = (f32[5,32,16,2]{1,2,3,0:T(8,128)S(1)}, f32[5,32,16,2]{1,2,3,0:T(8,128)S(1)}, u32[]{:S(2)}, u32[]{:S(2)}) collective-permute-start(f32[5,32,16,2]{1,2,3,0:T(8,128)S(1)} %copy.26), channel_id=1, source_target_pairs={{1,0},{2,1},{3,2},{4,3},{5,4},{6,5},{7,6},{8,7},{9,8},{10,9},{11,1... | collective-permute-start | bytes 61448 | tf_op jit(solution)/shard_map/ppermute | solution.py:298
  171.3 2.1 %pad_maximum_fusion.1.s_ref = f32[2,32,16,256]{3,2,1,0:T(8,128)} fusion(f32[1,32,16,256]{3,2,1,0:T(8,128)} %get-tuple-element.7, f32[1,32,16,256]{3,2,1,0:T(8,128)S(1)} %get-tuple-element.6), kind=kLoop, calls=%fused_computation.33 | loop fusion | flops 262144 | bytes 2097152 | tf_op jit(solution)/shard_map/stack | solution.py:281
  173.5 1.6 copy.28.ah_ref
  175.1 1.6 copy.27.al_ref
  176.7 15.6 %shard_map.87 = f32[5,32,16,256]{3,2,1,0:T(8,128)} custom-call(f32[5,32,16,256]{3,2,1,0:T(8,128)} %copy-done, f32[2,32,16,256]{3,2,1,0:T(8,128)} %pad_maximum_fusion.1.s_ref, f32[5,2,16,256]{3,2,1,0:T(8,128)} %collective-permute-done.rl_ref, f32[5,2,16,256]{3,2,1,0:T(8,128)} %collective-permute-done.1.rh_ref, f32[5,32,16,2]{3,2,1,0:T(8,128)} %copy.27.al_ref, ...), custom_call_target="tpu_custom_call" | custom-call | tf_op jit(solution)/shard_map/pallas_call | solution.py:182
  (43 shorter events, 3.0 us)
Async XLA Ops:
  4.1 9.9 %copy-start.4 = (s32[4096]{0:T(1024)S(1)}, s32[4096]{0:T(1024)}, u32[]{:S(2)}) copy-start(s32[4096]{0:T(1024)} %param.12) | copy-start | bytes 49156
  4.1 10.0 %copy-start.3 = (s32[4096,1]{0,1:T(1,128)S(1)}, s32[4096,1]{0,1:T(1,128)}, u32[]{:S(2)}) copy-start(s32[4096,1]{0,1:T(1,128)} %param.13) | copy-start | bytes 49156
  4.1 44.3 %all-to-all-start = ((f32[32,5,16,256]{3,2,1,0:T(8,128)}), f32[32,5,16,256]{3,2,1,0:T(8,128)S(1)}, u32[]{:S(2)}, u32[]{:S(2)}) async-start(f32[32,5,16,256]{3,2,1,0:T(8,128)} %bitcast.83), calls=%async_computation | async-start | bytes 5242880 | tf_op jit(solution)/shard_map/all_to_all | solution.py:204
  14.1 1.4 copy-start.2
  14.1 1.4 copy-start.5
  14.1 1.4 copy-start.6
  15.7 42.6 %copy-start.7 = (s32[32]{0:T(128)S(1)}, s32[32]{0:T(128)}, u32[]{:S(2)}) copy-start(s32[32]{0:T(128)} %param.8) | copy-start | bytes 388
  48.4 13.1 %copy-start.1 = (f32[32,5,16,256]{3,2,1,0:T(8,128)}, f32[32,5,16,256]{3,2,1,0:T(8,128)S(1)}, u32[]{:S(2)}) copy-start(f32[32,5,16,256]{3,2,1,0:T(8,128)S(1)} %all-to-all-done) | copy-start | bytes 7864324
  49.9 18.5 %all-to-all-start.2 = ((f32[128,1,384]{2,1,0:T(1,128)}), f32[128,1,384]{2,1,0:T(1,128)S(1)}, u32[]{:S(2)}, u32[]{:S(2)}) async-start(f32[128,1,384]{2,1,0:T(1,128)} %reshape.194), calls=%async_computation.2 | async-start | bytes 393216 | tf_op jit(solution)/shard_map/all_to_all | solution.py:246
  68.5 41.4 %all-to-all-start.1 = ((f32[32,5,16,256]{3,2,1,0:T(8,128)}), f32[32,5,16,256]{3,2,1,0:T(8,128)}, u32[]{:S(2)}, u32[]{:S(2)}) async-start(f32[32,5,16,256]{3,2,1,0:T(8,128)} %bitcast.82), calls=%async_computation.1 | async-start | bytes 5242880 | tf_op jit(solution)/shard_map/all_to_all | solution.py:209
  155.7 8.6 %copy-start = (f32[5,32,16,256]{3,2,1,0:T(8,128)}, f32[5,32,16,256]{3,2,1,0:T(8,128)S(1)}, u32[]{:S(2)}) copy-start(f32[5,32,16,256]{3,2,1,0:T(8,128)S(1)} %pad_maximum_fusion.d_ref) | copy-start | bytes 7864324
  155.8 20.9 %collective-permute-start.1 = (f32[5,2,16,256]{3,2,1,0:T(8,128)S(1)}, f32[5,2,16,256]{3,2,1,0:T(8,128)}, u32[]{:S(2)}, u32[]{:S(2)}) collective-permute-start(f32[5,2,16,256]{3,2,1,0:T(8,128)S(1)} %get-tuple-element.10), channel_id=1, source_target_pairs={{32,0},{64,32},{96,64},{33,1},{65,33},{97,65},{34,2},{66,34},{98,6... | collective-permute-start | bytes 491528 | tf_op jit(solution)/shard_map/ppermute | solution.py:288
  159.7 17.1 %collective-permute-start = (f32[5,2,16,256]{3,2,1,0:T(8,128)S(1)}, f32[5,2,16,256]{3,2,1,0:T(8,128)}, u32[]{:S(2)}, u32[]{:S(2)}) collective-permute-start(f32[5,2,16,256]{3,2,1,0:T(8,128)S(1)} %get-tuple-element.11), channel_id=1, source_target_pairs={{0,32},{32,64},{64,96},{1,33},{33,65},{65,97},{2,34},{34,66},{66,9... | collective-permute-start | bytes 491528 | tf_op jit(solution)/shard_map/ppermute | solution.py:283
  165.6 9.5 %collective-permute-start.2 = (f32[5,32,16,2]{1,2,3,0:T(8,128)S(1)}, f32[5,32,16,2]{1,2,3,0:T(8,128)S(1)}, u32[]{:S(2)}, u32[]{:S(2)}) collective-permute-start(f32[5,32,16,2]{1,2,3,0:T(8,128)S(1)} %copy.25), channel_id=1, source_target_pairs={{0,1},{1,2},{2,3},{3,4},{4,5},{5,6},{6,7},{7,8},{8,9},{9,10},{10,1... | collective-permute-start | bytes 61448 | tf_op jit(solution)/shard_map/ppermute | solution.py:293
  165.7 7.8 %collective-permute-start.3 = (f32[5,32,16,2]{1,2,3,0:T(8,128)S(1)}, f32[5,32,16,2]{1,2,3,0:T(8,128)S(1)}, u32[]{:S(2)}, u32[]{:S(2)}) collective-permute-start(f32[5,32,16,2]{1,2,3,0:T(8,128)S(1)} %copy.26), channel_id=1, source_target_pairs={{1,0},{2,1},{3,2},{4,3},{5,4},{6,5},{7,6},{8,7},{9,8},{10,9},{11,1... | collective-permute-start | bytes 61448 | tf_op jit(solution)/shard_map/ppermute | solution.py:298

commit v6 on v5

--- a/solution.py
+++ b/solution.py
@@ -123,10 +123,10 @@
     lower = flux(v_m1 + 0.5 * slope_m1, v0 - 0.5 * slope_0, 0.5 * (s_m1 + s0))
     return upper - lower
 
-def transport(dragged, speeds, radial_low, radial_high, ring_low, ring_high, rate_r, rate_a):
+def transport(dragged, radial_low, radial_high, ring_low, ring_high, rate_r, rate_a):
     fields, radii, layers, cells = dragged.shape
 
-    def kernel(d_ref, s_ref, rl_ref, rh_ref, al_ref, ah_ref, out_ref):
+    def kernel(d_ref, rl_ref, rh_ref, al_ref, ah_ref, out_ref):
         lane = lax.broadcasted_iota(jnp.int32, (layers, cells), 1)
 
         def edge_of(ref, f, component, *index):
@@ -138,7 +138,7 @@
 
         def radial_at(f, r, offset):
             k = r + offset
-            inner = d_ref[f, jnp.clip(k, 0, radii - 1)] if f < fields else s_ref[0, jnp.clip(k, 0, radii - 1)]
+            inner = d_ref[f, jnp.clip(k, 0, radii - 1)] if f < fields else d_ref[1, jnp.clip(k, 0, radii - 1)] / d_ref[0, jnp.clip(k, 0, radii - 1)]
             low = edge_of(rl_ref, f, 1, jnp.clip(k + 2, 0, 1))
             high = edge_of(rh_ref, f, 1, jnp.clip(k - radii, 0, 1))
             return jnp.where(k < 0, low, jnp.where(k >= radii, high, inner))
@@ -157,8 +157,8 @@
             return moved
 
         def body(r, carry):
-            sr = s_ref[0, r]
-            sa = s_ref[1, r]
+            sr = d_ref[1, r] / d_ref[0, r]
+            sa = d_ref[2, r] / d_ref[0, r]
             sr_m1 = radial_at(fields, r, -1)
             sr_p1 = radial_at(fields, r, 1)
             sa_m1 = ring_at(sa, fields + 1, r, -1)
@@ -182,9 +182,9 @@
     return pl.pallas_call(
         kernel,
         out_shape=jax.ShapeDtypeStruct(dragged.shape, dragged.dtype),
-        in_specs=[vmem] * 6,
+        in_specs=[vmem] * 5,
         out_specs=vmem,
-    )(dragged, speeds, radial_low, radial_high, ring_low, ring_high)
+    )(dragged, radial_low, radial_high, ring_low, ring_high)
 
 
 def local(
@@ -276,9 +276,6 @@
         .reshape(3, radius_count, layers, sector)
     )
     dragged = jnp.concatenate([shifted[0:1], shifted[1:4] + momentum_added, shifted[4:5]], axis=0)
-    radial_speed = dragged[1] / dragged[0]
-    azimuthal_speed = dragged[2] / dragged[0]
-    speeds = jnp.stack([radial_speed, azimuthal_speed], axis=0)
     rads = lax.axis_size("rad")
     radial_low = lax.ppermute(
         dragged[:, -2:],
@@ -301,7 +298,7 @@
         [((i + 1) % sectors, i) for i in range(sectors)],
     )
     gas_next = transport(
-        dragged, speeds, radial_low, radial_high, ring_low, ring_high, radial_rate, azimuth_rate
+        dragged, radial_low, radial_high, ring_low, ring_high, radial_rate, azimuth_rate
     )
     return (gas_next, arrived_velocity)
 

time: 193 us -> 196 us (1.016)
  waiting for transfers between devices: 55.4 us -> 61.3 us
  other arithmetic: 13.6 us -> 10.5 us
  local copies, waits for them, and re-layouts: 17.2 us -> 19.4 us
  starting transfers between devices: 40.5 us -> 38.4 us
    ppermute x1, waiting for transfers between devices: 0.01 us -> 5.08 us  [local(): lax.ppermute(dragged[..., -2:], 'sec', [(i, (i + 1) % sectors) for i in r...]
    another operation x1 -> x0, other arithmetic: 2.11 us -> none  [local(): speeds = jnp.stack([radial_speed, azimuthal_speed], axis=0)]
    ppermute x1, starting transfers between devices: 5.67 us -> 3.57 us  [local(): lax.ppermute(dragged[..., :2], 'sec', [((i + 1) % sectors, i) for i in ra...]
    unnamed x19 -> x25, local copies, waits for them, and re-layouts: 4.92 us -> 6.28 us
  transfers between devices with their start and end apart: 7 -> 7, of which waited for: 3 -> 5; matrix products, arithmetic and copies ran while one was open for 10% -> 9% of each run, Pallas kernels for 3% -> 3%
where the time goes in v6:
time: 196 us; the launch traced here: 195 us
  waiting for transfers between devices  61.3 us (31%)
  matrix products  39.8 us (20%)
  starting transfers between devices  38.4 us (20%)
  Pallas kernels  22.1 us (11%)
  local copies, waits for them, and re-layouts  19.4 us (10%)
  other arithmetic  10.5 us (5%)
  between operations  3.57 us (2%)
    all_to_all x1, waiting for transfers between devices, local(): lax.all_to_all(by_radius, 'sec', split_axis=0, concat_axis=0, tiled=True)  29.1 us
    all_to_all x1, waiting for transfers between devices, local(): lax.all_to_all(rolled, 'sec', split_axis=0, concat_axis=0, tiled=True)  26 us
    dot_general x1, matrix products, local(): jnp.dot(row_hot.T, spread, precision=lax.Precision.HIGH, preferred_elemen...  18.3 us
    dot_general x1, matrix products, local(): jnp.dot(row_hot, velocity_rows, precision=lax.Precision.HIGH, preferred_e...  17 us
    pallas_call x1, Pallas kernels, transport(): pl.pallas_call(kernel, out_shape=jax.ShapeDtypeStruct(dragged.shape, drag...  15.4 us
    all_to_all x1, starting transfers between devices, local(): lax.all_to_all(by_radius, 'sec', split_axis=0, concat_axis=0, tiled=True)  9.93 us
    all_to_all x1, starting transfers between devices, local(): lax.all_to_all(rolled, 'sec', split_axis=0, concat_axis=0, tiled=True)  8.38 us
    all_to_all x1, starting transfers between devices, local(): lax.all_to_all(outbox, ('rad', 'sec'), split_axis=0, concat_axis=0, tiled...  8.35 us
  transfers between devices with their start and end apart: 7, of which 5 were waited for; matrix products, arithmetic and copies ran while one was open for 9% of the time, Pallas kernels for 3%

profile of v6, /device:TPU:1, one launch (start us, length us, event | category | flops | bytes accessed | tf_op | source)
XLA Modules:
  0.0 195.1 jit_solution(15025727036076412054)
XLA Ops:
  0.6 3.5 %copy.34 = f32[5,32,16,256]{3,2,0,1:T(8,128)} copy(f32[5,32,16,256]{3,2,1,0:T(8,128)} %param.7) | data formatting | bytes 5242880 | tf_op args[0]
  4.1 9.9 %all-to-all-start = ((f32[32,5,16,256]{3,2,1,0:T(8,128)}), f32[32,5,16,256]{3,2,1,0:T(8,128)S(1)}, u32[]{:S(2)}, u32[]{:S(2)}) async-start(f32[32,5,16,256]{3,2,1,0:T(8,128)} %bitcast.82), calls=%async_computation | async-start | bytes 5242880 | tf_op jit(solution)/shard_map/all_to_all | solution.py:204
  14.6 0.8 fusion.18
  15.7 3.5 %fusion.12 = f32[128,6,64]{0,2,1:T(8,128)S(1)} fusion(f32[4096,6]{0,1:T(8,128)S(1)} %maximum_bitcast_fusion, pred[4096,64]{0,1:T(8,128)(4,1)S(1)} %iota_compare_fusion.7, s32[4096]{0:T(1024)S(1)} %bitcast.91), kind=kOutput, calls=%fused_computation.13 | convolution fusion | flops 2418016256 | bytes 573440 | tf_op jit(solution)/shard_map/dot_general | solution.py:242
  19.3 29.1 %all-to-all-done = f32[32,5,16,256]{3,2,1,0:T(8,128)S(1)} async-done(((f32[32,5,16,256]{3,2,1,0:T(8,128)}), f32[32,5,16,256]{3,2,1,0:T(8,128)S(1)}, u32[]{:S(2)}, u32[]{:S(2)}) %all-to-all-start) | async-done | bytes 2621472 | tf_op jit(solution)/shard_map/all_to_all | solution.py:204
  48.7 1.3 reshape.194
  49.9 8.3 %all-to-all-start.2 = ((f32[128,1,384]{2,1,0:T(1,128)}), f32[128,1,384]{2,1,0:T(1,128)S(1)}, u32[]{:S(2)}, u32[]{:S(2)}) async-start(f32[128,1,384]{2,1,0:T(1,128)} %reshape.194), calls=%async_computation.2 | async-start | bytes 393216 | tf_op jit(solution)/shard_map/all_to_all | solution.py:246
  61.5 6.7 %shard_map.86 = f32[32,1,80,256]{3,2,1,0:T(8,128)} custom-call(s32[1]{0:T(128)S(6)} %select_n.48.quotient_ref, s32[1]{0:T(128)S(6)} %select_n.49.remainder_ref, f32[32,1,80,256]{3,2,1,0:T(8,128)} %bitcast.80), custom_call_target="tpu_custom_call" | custom-call | tf_op jit(solution)/shard_map/pallas_call | solution.py:101
  68.5 8.4 %all-to-all-start.1 = ((f32[32,5,16,256]{3,2,1,0:T(8,128)}), f32[32,5,16,256]{3,2,1,0:T(8,128)}, u32[]{:S(2)}, u32[]{:S(2)}) async-start(f32[32,5,16,256]{3,2,1,0:T(8,128)} %bitcast.81), calls=%async_computation.1 | async-start | bytes 5242880 | tf_op jit(solution)/shard_map/all_to_all | solution.py:209
  77.4 1.1 reduce.14
  79.8 4.2 %fusion.11 = f32[8192,256]{0,1:T(8,128)} fusion(s32[8192]{0:T(1024)S(1)} %get-tuple-element.16), kind=kLoop, calls=%fused_computation.12 | loop fusion | flops 4194304 | bytes 8421376 | tf_op jit(solution)/shard_map/convert_element_type | solution.py:261
  84.0 26.0 %all-to-all-done.1 = f32[32,5,16,256]{3,2,1,0:T(8,128)} async-done(((f32[32,5,16,256]{3,2,1,0:T(8,128)}), f32[32,5,16,256]{3,2,1,0:T(8,128)}, u32[]{:S(2)}, u32[]{:S(2)}) %all-to-all-start.1) | async-done | bytes 2621472 | tf_op jit(solution)/shard_map/all_to_all | solution.py:209
  109.9 2.1 %copy.33 = f32[32,5,16,256]{3,2,0,1:T(8,128)S(1)} copy(f32[32,5,16,256]{3,2,1,0:T(8,128)} %all-to-all-done.1) | data formatting | bytes 5242880 | tf_op jit(solution)/shard_map/all_to_all | solution.py:209
  112.0 0.9 fusion.42
  112.9 1.4 slice_divide_fusion
  114.3 3.1 %copy.23 = f32[3,512,256]{1,2,0:T(8,128)} copy(f32[3,512,256]{2,1,0:T(8,128)} %bitcast.83) | data formatting | bytes 3145728 | tf_op jit(solution)/shard_map/reshape | solution.py:251
  117.4 17.0 %multiply_reduce_fusion = f32[8192,3]{0,1:T(4,128)S(1)} fusion(f32[8192,256]{0,1:T(8,128)} %fusion.11, f32[3,512,256]{1,2,0:T(8,128)} %copy.23, s32[8192]{0:T(1024)S(1)} %get-tuple-element.15), kind=kOutput, calls=%fused_computation.3 | convolution fusion | flops 19344105472 | bytes 10092544 | tf_op jit(solution)/shard_map/dot_general | solution.py:262
  134.4 0.7 fusion.32
  135.1 18.3 %fusion = f32[512,3,256]{2,0,1:T(8,128)} fusion(f32[8192,3]{0,1:T(4,128)S(1)} %get-tuple-element.14, f32[8192,256]{0,1:T(8,128)} %fusion.11, s32[8192]{0:T(1024)S(1)} %get-tuple-element.15), kind=kOutput, calls=%fused_computation | convolution fusion | flops 19337838592 | bytes 10092544 | tf_op jit(solution)/shard_map/dot_general | solution.py:272
  153.4 1.8 slice_add_fusion
  155.7 3.9 %collective-permute-start.1 = (f32[5,2,16,256]{3,2,1,0:T(8,128)S(1)}, f32[5,2,16,256]{3,2,1,0:T(8,128)S(1)}, u32[]{:S(2)}, u32[]{:S(2)}) collective-permute-start(f32[5,2,16,256]{3,2,1,0:T(8,128)S(1)} %get-tuple-element.8), channel_id=1, source_target_pairs={{32,0},{64,32},{96,64},{33,1},{65,33},{97,65},{34,2},{66,34},{98,6... | collective-permute-start | bytes 491528 | tf_op jit(solution)/shard_map/ppermute | solution.py:285
  159.6 4.2 %collective-permute-start = (f32[5,2,16,256]{3,2,1,0:T(8,128)S(1)}, f32[5,2,16,256]{3,2,1,0:T(8,128)S(1)}, u32[]{:S(2)}, u32[]{:S(2)}) collective-permute-start(f32[5,2,16,256]{3,2,1,0:T(8,128)S(1)} %get-tuple-element.9), channel_id=1, source_target_pairs={{0,32},{32,64},{64,96},{1,33},{33,65},{65,97},{2,34},{34,66},{66,9... | collective-permute-start | bytes 491528 | tf_op jit(solution)/shard_map/ppermute | solution.py:280
  164.3 0.6 copy.26
  164.9 3.6 %collective-permute-start.3 = (f32[5,32,16,2]{1,2,3,0:T(8,128)S(1)}, f32[5,32,16,2]{1,2,3,0:T(8,128)S(1)}, u32[]{:S(2)}, u32[]{:S(2)}) collective-permute-start(f32[5,32,16,2]{1,2,3,0:T(8,128)S(1)} %copy.26), channel_id=1, source_target_pairs={{1,0},{2,1},{3,2},{4,3},{5,4},{6,5},{7,6},{8,7},{9,8},{10,9},{11,1... | collective-permute-start | bytes 61448 | tf_op jit(solution)/shard_map/ppermute | solution.py:295
  168.5 0.6 copy.25
  169.1 0.8 collective-permute-done.3
  169.9 1.6 copy.28.ah_ref
  171.6 5.1 %collective-permute-done.2 = f32[5,32,16,2]{1,2,3,0:T(8,128)S(1)} collective-permute-done((f32[5,32,16,2]{1,2,3,0:T(8,128)S(1)}, f32[5,32,16,2]{1,2,3,0:T(8,128)S(1)}, u32[]{:S(2)}, u32[]{:S(2)}) %collective-permute-start.2) | collective-permute-done | bytes 20512 | tf_op jit(solution)/shard_map/ppermute | solution.py:290
  176.6 1.6 copy.27.al_ref
  178.3 0.7 copy-done.3
  178.9 0.7 copy-done.4
  179.6 15.4 %shard_map.87 = f32[5,32,16,256]{3,2,1,0:T(8,128)} custom-call(f32[5,32,16,256]{3,2,1,0:T(8,128)} %copy-done, f32[5,2,16,256]{3,2,1,0:T(8,128)} %copy-done.4, f32[5,2,16,256]{3,2,1,0:T(8,128)} %copy-done.3, f32[5,32,16,2]{3,2,1,0:T(8,128)} %copy.27.al_ref, f32[5,32,16,2]{3,2,1,0:T(8,128)} %copy.28.ah_ref), custom_call_target="tpu_custom_call" | custom-call | tf_op jit(solution)/shard_map/pallas_call | solution.py:182
  (47 shorter events, 4.5 us)
Async XLA Ops:
  4.1 9.9 %copy-start.7 = (s32[4096]{0:T(1024)S(1)}, s32[4096]{0:T(1024)}, u32[]{:S(2)}) copy-start(s32[4096]{0:T(1024)} %param.12) | copy-start | bytes 49156
  4.1 10.0 %copy-start.6 = (s32[4096,1]{0,1:T(1,128)S(1)}, s32[4096,1]{0,1:T(1,128)}, u32[]{:S(2)}) copy-start(s32[4096,1]{0,1:T(1,128)} %param.13) | copy-start | bytes 49156
  4.1 44.3 %all-to-all-start = ((f32[32,5,16,256]{3,2,1,0:T(8,128)}), f32[32,5,16,256]{3,2,1,0:T(8,128)S(1)}, u32[]{:S(2)}, u32[]{:S(2)}) async-start(f32[32,5,16,256]{3,2,1,0:T(8,128)} %bitcast.82), calls=%async_computation | async-start | bytes 5242880 | tf_op jit(solution)/shard_map/all_to_all | solution.py:204
  14.1 1.4 copy-start.5
  14.1 1.4 copy-start.8
  14.1 1.4 copy-start.9
  15.7 42.6 %copy-start.10 = (s32[32]{0:T(128)S(1)}, s32[32]{0:T(128)}, u32[]{:S(2)}) copy-start(s32[32]{0:T(128)} %param.8) | copy-start | bytes 388
  48.4 13.1 %copy-start.1 = (f32[32,5,16,256]{3,2,1,0:T(8,128)}, f32[32,5,16,256]{3,2,1,0:T(8,128)S(1)}, u32[]{:S(2)}) copy-start(f32[32,5,16,256]{3,2,1,0:T(8,128)S(1)} %all-to-all-done) | copy-start | bytes 7864324
  49.9 18.5 %all-to-all-start.2 = ((f32[128,1,384]{2,1,0:T(1,128)}), f32[128,1,384]{2,1,0:T(1,128)S(1)}, u32[]{:S(2)}, u32[]{:S(2)}) async-start(f32[128,1,384]{2,1,0:T(1,128)} %reshape.194), calls=%async_computation.2 | async-start | bytes 393216 | tf_op jit(solution)/shard_map/all_to_all | solution.py:246
  68.5 41.4 %all-to-all-start.1 = ((f32[32,5,16,256]{3,2,1,0:T(8,128)}), f32[32,5,16,256]{3,2,1,0:T(8,128)}, u32[]{:S(2)}, u32[]{:S(2)}) async-start(f32[32,5,16,256]{3,2,1,0:T(8,128)} %bitcast.81), calls=%async_computation.1 | async-start | bytes 5242880 | tf_op jit(solution)/shard_map/all_to_all | solution.py:209
  153.4 1.8 copy-start.2
  155.6 8.6 %copy-start = (f32[5,32,16,256]{3,2,1,0:T(8,128)}, f32[5,32,16,256]{3,2,1,0:T(8,128)S(1)}, u32[]{:S(2)}) copy-start(f32[5,32,16,256]{3,2,1,0:T(8,128)S(1)} %pad_maximum_fusion.d_ref) | copy-start | bytes 7864324
  155.7 22.6 %collective-permute-start.1 = (f32[5,2,16,256]{3,2,1,0:T(8,128)S(1)}, f32[5,2,16,256]{3,2,1,0:T(8,128)S(1)}, u32[]{:S(2)}, u32[]{:S(2)}) collective-permute-start(f32[5,2,16,256]{3,2,1,0:T(8,128)S(1)} %get-tuple-element.8), channel_id=1, source_target_pairs={{32,0},{64,32},{96,64},{33,1},{65,33},{97,65},{34,2},{66,34},{98,6... | collective-permute-start | bytes 491528 | tf_op jit(solution)/shard_map/ppermute | solution.py:285
  159.6 18.7 %collective-permute-start = (f32[5,2,16,256]{3,2,1,0:T(8,128)S(1)}, f32[5,2,16,256]{3,2,1,0:T(8,128)S(1)}, u32[]{:S(2)}, u32[]{:S(2)}) collective-permute-start(f32[5,2,16,256]{3,2,1,0:T(8,128)S(1)} %get-tuple-element.9), channel_id=1, source_target_pairs={{0,32},{32,64},{64,96},{1,33},{33,65},{65,97},{2,34},{34,66},{66,9... | collective-permute-start | bytes 491528 | tf_op jit(solution)/shard_map/ppermute | solution.py:280
  164.9 5.1 %collective-permute-start.3 = (f32[5,32,16,2]{1,2,3,0:T(8,128)S(1)}, f32[5,32,16,2]{1,2,3,0:T(8,128)S(1)}, u32[]{:S(2)}, u32[]{:S(2)}) collective-permute-start(f32[5,32,16,2]{1,2,3,0:T(8,128)S(1)} %copy.26), channel_id=1, source_target_pairs={{1,0},{2,1},{3,2},{4,3},{5,4},{6,5},{7,6},{8,7},{9,8},{10,9},{11,1... | collective-permute-start | bytes 61448 | tf_op jit(solution)/shard_map/ppermute | solution.py:295
  169.1 7.6 %collective-permute-start.2 = (f32[5,32,16,2]{1,2,3,0:T(8,128)S(1)}, f32[5,32,16,2]{1,2,3,0:T(8,128)S(1)}, u32[]{:S(2)}, u32[]{:S(2)}) collective-permute-start(f32[5,32,16,2]{1,2,3,0:T(8,128)S(1)} %copy.25), channel_id=1, source_target_pairs={{0,1},{1,2},{2,3},{3,4},{4,5},{5,6},{6,7},{7,8},{8,9},{9,10},{10,1... | collective-permute-start | bytes 61448 | tf_op jit(solution)/shard_map/ppermute | solution.py:290
  178.3 0.7 copy-start.3
  178.9 0.7 copy-start.4
